TPU v7x, 256 devices: a whole 4x4x8 slice. The times are simulated.
256 devices in a mesh: samp: 32 (over x, z), snp: 8 (over y, core).
Axes of the slice: x: 4, y: 4, z: 8, core: 2. Of those that a mesh axis runs over, the one named last changes fastest.
Arguments:
- dosages: float32 [49152, 8192], P('samp', 'snp'), as said below
- band_counts: int32 [16], P('snp'), may hold values from 1 to 4, as said below
Outputs:
- corr_tiles: float32 [512, 16, 4, 512], P('samp', 'snp')
Inputs may be any that keep to these rules, and one draw needn't show every extreme that they name: b + band_counts[b] <= 16 for every block b, and the counts of all blocks sum to exactly 32. `dosages`: finite real values.
All inputs are finite; a program needn't handle non-finite values.
Results may differ from a plain program's by a relative error of at most 0.0001.
Values sent between devices are 32-bit elements; how exact they have to be, the bound alone decides.
No kernel may reach another device: no remote copies, remote signals or barrier semaphores. Data moves between devices by JAX's collectives and lax.ppermute only.
A program may use at most 192 MiB of HBM per device.

v0:
```python
import jax
import jax.numpy as jnp
from jax import lax
from jax.sharding import PartitionSpec as P

MAXBAND = 4


HIGHEST_MODE = lax.Precision.HIGH
epsilon_value = 1e-06
transposed_dims = (((0,), (0,)), ((), ()))


def shifted(value, axis, steps):
    count = lax.axis_size(axis)
    first, last = (max(0, -steps), min(count, count - steps))
    return lax.ppermute(value, axis, [(source, source + steps) for source in range(first, last)])


def ring_steps(piece_of, axis, count):
    me = lax.axis_index(axis)
    forward = [(i, (i + 1) % count) for i in range(count)]
    backward = [(i, (i - 1) % count) for i in range(count)]
    up = piece_of(me - 1 + count, 0)
    down = piece_of(me + 1, 1)
    for step in range(count - 1):
        up, down = lax.optimization_barrier((up, down))
        up = lax.ppermute(up, axis, forward) + piece_of(me - step - 2 + 2 * count, 0)
        down = lax.ppermute(down, axis, backward) + piece_of(me + step + 2, 1)
    return jnp.concatenate([up, down], axis=-1)


def ring_reduce_scatter(tiles, major, minor):
    major_count = lax.axis_size(major)
    minor_count = lax.axis_size(minor)
    rows = tiles[0].shape[0] // (major_count * minor_count)
    half = tiles[0].shape[-1] // 2
    grouped = [t.reshape((major_count, minor_count, rows) + t.shape[1:]) for t in tiles]

    def first_piece(index, part):
        pieces = [lax.dynamic_index_in_dim(g, index % minor_count, 1, keepdims=False) for g in grouped]
        pieces = [p[..., :half] if part == 0 else p[..., half:] for p in pieces]
        return jnp.stack(pieces, axis=2)

    partial = ring_steps(first_piece, minor, minor_count)

    def second_piece(index, part):
        piece = lax.dynamic_index_in_dim(partial, index % major_count, 0, keepdims=False)
        return piece[..., :half] if part == 0 else piece[..., half:]

    return ring_steps(second_piece, major, major_count)


def samp_size():
    return lax.axis_size("samp_x") * lax.axis_size("samp_z")


def samp_sum(value):
    return lax.psum(lax.psum(value, "samp_z"), "samp_x")


def on_device(dosages, band_counts):
    samp_rows, column_total = dosages.shape
    blocks_here = band_counts.shape[0]
    block_width = column_total // blocks_here
    band_limit = MAXBAND
    sample_total = samp_rows * samp_size()
    inverse_total = 1.0 / sample_total

    reach = (band_limit - 1 + blocks_here - 1) // blocks_here
    widths = [column_total]
    raw_sources = [dosages]
    for offset in range(1, reach + 1):
        last_block = min(band_limit - 1 + blocks_here - 1, offset * blocks_here + blocks_here - 1)
        need = (last_block - offset * blocks_here + 1) * block_width
        widths.append(need)
    raw_sources.append(shifted(dosages[:, : widths[1]], "snp", -1))
    snp_count = lax.axis_size("snp")
    far = lax.ppermute(dosages[:, : widths[2]], "snp", [(j + 2, j) for j in range(1, snp_count - 2, 2)])
    near = lax.ppermute(raw_sources[1][:, : widths[2]], "snp", [(j + 1, j) for j in range(0, snp_count - 1, 2)])
    raw_sources.append(far + near)

    column_sum = samp_sum(jnp.sum(dosages, axis=0))
    center = column_sum * inverse_total
    deviation = dosages - center
    square_sum = samp_sum(jnp.sum(deviation * deviation, axis=0))
    spread = square_sum * inverse_total
    inverse_sd = 1.0 / jnp.sqrt(spread + epsilon_value)

    stats = jnp.stack([center, inverse_sd])
    scales = [inverse_sd]
    sources = [deviation]
    for offset in range(1, reach + 1):
        width = widths[offset]
        moved = shifted(stats[:, :width], "snp", -offset)
        scales.append(moved[1])
        sources.append(raw_sources[offset] - moved[0])

    def tile(local_block, band_index):
        column_block = local_block + band_index
        source = sources[column_block // blocks_here]
        column_start = column_block % blocks_here * block_width
        left_panel = deviation[:, local_block * block_width : (local_block + 1) * block_width]
        right_panel = source[:, column_start : column_start + block_width]
        return lax.dot_general(
            left_panel,
            right_panel,
            transposed_dims,
            precision=HIGHEST_MODE,
            preferred_element_type=jnp.float32,
        )

    band_range = jnp.arange(band_limit, dtype=jnp.int32)
    live_mask = band_range[None, :] < band_counts[:, None]
    tiles = [tile(local_block, band_index) for local_block in range(blocks_here) for band_index in range(band_limit)]
    summed = ring_reduce_scatter(tiles, "samp_x", "samp_z")
    reduced = summed.reshape((summed.shape[0], blocks_here, band_limit, summed.shape[-1]))

    own_rows = block_width // samp_size()
    row_start = (lax.axis_index("samp_x") * lax.axis_size("samp_z") + lax.axis_index("samp_z")) * own_rows
    row_list = []
    for local_block in range(blocks_here):
        row_scale = lax.dynamic_slice_in_dim(inverse_sd, local_block * block_width + row_start, own_rows)
        band_list = []
        for band_index in range(band_limit):
            column_block = local_block + band_index
            source_scale = scales[column_block // blocks_here]
            column_start = column_block % blocks_here * block_width
            column_scale = source_scale[column_start : column_start + block_width]
            scaled_tile = reduced[:, local_block, band_index] * row_scale[:, None] * column_scale[None, :] * inverse_total
            band_list.append(jnp.where(live_mask[local_block, band_index], scaled_tile, 0.0))
        row_list.append(jnp.stack(band_list, axis=1))
    return jnp.stack(row_list, axis=1)


def solution(mesh):
    x_size = mesh.devices.shape[0] // 8 if mesh.devices.shape[0] % 8 == 0 else 1
    split = jax.sharding.Mesh(
        mesh.devices.reshape(x_size, mesh.devices.shape[0] // x_size, mesh.devices.shape[1]),
        ("samp_x", "samp_z", "snp"),
    )
    return jax.shard_map(
        on_device,
        mesh=split,
        in_specs=(P(("samp_x", "samp_z"), "snp"), P("snp")),
        out_specs=P(("samp_x", "samp_z"), "snp", None, None),
        check_vma=False,
    )
```

profile of v0, /device:TPU:8, one launch (start us, length us, event | category | flops | bytes accessed | tf_op | source)
XLA Modules:
  0.0 286.5 jit_solution(16302621108121474093)
XLA Ops:
  0.0 1.9 collective-permute-start
  1.9 3.2 %reduce_sum.18 = f32[1024]{0:T(1024)S(1)} reduce(f32[1536,1024]{1,0:T(8,128)} %param.2, f32[]{:T(128)} %constant.672.clone.1), dimensions={0}, to_apply=%region_0.0 | reduce | flops 1571840 | bytes 6295556 | tf_op jit(solution)/shard_map/reduce_sum | solution.py:83
  5.1 20.0 %psum.28 = f32[1024]{0:T(1024)S(1)} all-reduce(f32[1024]{0:T(1024)S(1)} %reduce_sum.18), channel_id=1, replica_groups=mesh['samp_x'=4,'samp_z'=8,'snp'=8] {'samp_z'}, use_global_device_ids=true, to_apply=%region_1.0 | all-reduce | flops 1024 | bytes 8192 | tf_op jit(solution)/shard_map/psum | solution.py:59
  25.1 10.5 %psum.29 = f32[1024]{0:T(1024)S(1)} all-reduce(f32[1024]{0:T(1024)S(1)} %psum.28), channel_id=1, replica_groups=mesh['samp_x'=4,'samp_z'=8,'snp'=8] {'samp_x'}, use_global_device_ids=true, to_apply=%region_2.0 | all-reduce | flops 1024 | bytes 8192 | tf_op jit(solution)/shard_map/psum | solution.py:59
  35.6 6.6 %multiply_reduce_fusion = (f32[1024]{0:T(1024)S(1)}, f32[1536,1024]{1,0:T(8,128)}) fusion(f32[1536,1024]{1,0:T(8,128)} %param.2, f32[1024]{0:T(1024)S(1)} %broadcast_multiply_fusion), kind=kLoop, calls=%fused_computation | loop fusion | flops 4717568 | bytes 12591104 | tf_op jit(solution)/shard_map/reduce_sum | solution.py:86
  42.2 14.1 %psum.30 = f32[1024]{0:T(1024)S(1)} all-reduce(f32[1024]{0:T(1024)S(1)} %get-tuple-element.45), channel_id=1, replica_groups=mesh['samp_x'=4,'samp_z'=8,'snp'=8] {'samp_z'}, use_global_device_ids=true, to_apply=%region_4.0 | all-reduce | flops 1024 | bytes 8192 | tf_op jit(solution)/shard_map/psum | solution.py:59
  56.4 7.7 %psum.31 = f32[1024]{0:T(1024)S(1)} all-reduce(f32[1024]{0:T(1024)S(1)} %psum.30), channel_id=1, replica_groups=mesh['samp_x'=4,'samp_z'=8,'snp'=8] {'samp_x'}, use_global_device_ids=true, to_apply=%region_5.0 | all-reduce | flops 1024 | bytes 8192 | tf_op jit(solution)/shard_map/psum | solution.py:59
  64.7 1.9 collective-permute-start.1
  66.7 1.9 collective-permute-start.4
  68.6 3.8 %slice.536 = f32[1536,512]{1,0:T(8,128)} slice(f32[1536,1024]{1,0:T(8,128)} %param.2), slice={[0:1536], [0:512]} | slice | bytes 6291456 | tf_op jit(solution)/shard_map/slice | solution.py:79
  72.4 2.5 collective-permute-start.2
  75.1 5.5 %fusion.15 = f32[512,512]{1,0:T(8,128)S(1)} fusion(f32[1536,1024]{1,0:T(8,128)} %get-tuple-element.46), kind=kOutput, calls=%fused_computation.18 | convolution fusion | flops 2415919104 | bytes 4194304 | tf_op jit(solution)/shard_map/dot_general | solution.py:105
  80.6 5.5 %fusion.13 = f32[512,512]{1,0:T(8,128)S(1)} fusion(f32[1536,1024]{1,0:T(8,128)} %get-tuple-element.46), kind=kOutput, calls=%fused_computation.16 | convolution fusion | flops 2415919104 | bytes 7340032 | tf_op jit(solution)/shard_map/dot_general | solution.py:105
  86.1 1.5 dynamic-slice_bitcast_fusion.6
  117.6 5.6 %fusion.20 = f32[512,512]{1,0:T(8,128)S(1)} fusion(f32[1536,1024]{1,0:T(8,128)} %get-tuple-element.46), kind=kOutput, calls=%fused_computation.23 | convolution fusion | flops 2415919104 | bytes 4194304 | tf_op jit(solution)/shard_map/dot_general | solution.py:105
  124.1 3.7 %broadcast_subtract_fusion = f32[1536,1024]{1,0:T(8,128)S(1)} fusion(f32[1536,1024]{1,0:T(8,128)} %collective-permute-done, f32[1024]{0:T(1024)S(1)} %bitcast.886), kind=kLoop, calls=%fused_computation.4 | loop fusion | flops 1572864 | bytes 12587008 | tf_op jit(solution)/shard_map/sub | solution.py:97
  128.1 3.0 %fusion.9 = f32[512,512]{1,0:T(8,128)S(1)} fusion(f32[1536,1024]{1,0:T(8,128)S(1)} %broadcast_subtract_fusion, f32[1536,1024]{1,0:T(8,128)S(1)} %bitcast.871), kind=kOutput, calls=%fused_computation.12 | convolution fusion | flops 2415919104 | bytes 7340032 | tf_op jit(solution)/shard_map/dot_general | solution.py:105
  131.1 2.8 fusion.5
  133.9 2.8 fusion.7
  136.6 2.2 slice.704
  138.8 1.7 collective-permute-start.3
  147.4 2.8 fusion.3
  150.2 4.7 %fusion = f32[512,512]{1,0:T(8,128)S(1)} fusion(f32[1536,512]{1,0:T(8,128)} %collective-permute-done.2, f32[1536,512]{1,0:T(8,128)S(1)} %collective-permute-done.3, f32[1536,1024]{1,0:T(8,128)S(1)} %bitcast.871, f32[512]{0:T(512)S(1)} %bitcast.890), kind=kOutput, calls=%fused_computation.1 | convolution fusion | flops 2417491968 | bytes 10487808 | tf_op jit(solution)/shard_map/dot_general | solution.py:105
  156.9 2.0 collective-permute-start.6
  159.0 12.1 %collective-permute-done.6 = f32[4,16,8,256]{3,1,0,2:T(8,128)S(1)} collective-permute-done((f32[4,16,8,256]{3,1,0,2:T(8,128)S(1)}, f32[4,16,8,256]{3,1,0,2:T(8,128)S(1)}, u32[]{:S(2)}, u32[]{:S(2)}) %collective-permute-start.6) | collective-permute-done | bytes 524320 | tf_op jit(solution)/shard_map/ppermute | solution.py:29
  171.2 3.9 %collective-permute-done.5 = f32[4,16,8,256]{3,1,0,2:T(8,128)S(1)} collective-permute-done((f32[4,16,8,256]{3,1,0,2:T(8,128)}, f32[4,16,8,256]{3,1,0,2:T(8,128)S(1)}, u32[]{:S(2)}, u32[]{:S(2)}) %collective-permute-start.5) | collective-permute-done | bytes 524320 | tf_op jit(solution)/shard_map/ppermute | solution.py:28
  175.2 2.0 collective-permute-start.7
  177.3 11.9 %collective-permute-done.8 = f32[4,16,8,256]{3,1,0,2:T(8,128)S(1)} collective-permute-done((f32[4,16,8,256]{3,1,0,2:T(8,128)S(1)}, f32[4,16,8,256]{3,1,0,2:T(8,128)S(1)}, u32[]{:S(2)}, u32[]{:S(2)}) %collective-permute-start.8) | collective-permute-done | bytes 524320 | tf_op jit(solution)/shard_map/ppermute | solution.py:29
  191.1 1.7 collective-permute-start.9
  192.8 11.0 %collective-permute-done.10 = f32[4,16,8,256]{3,1,0,2:T(8,128)S(1)} collective-permute-done((f32[4,16,8,256]{3,1,0,2:T(8,128)S(1)}, f32[4,16,8,256]{3,1,0,2:T(8,128)S(1)}, u32[]{:S(2)}, u32[]{:S(2)}) %collective-permute-start.10) | collective-permute-done | bytes 524320 | tf_op jit(solution)/shard_map/ppermute | solution.py:29
  205.9 1.6 collective-permute-start.11
  207.6 10.2 %collective-permute-done.12 = f32[4,16,8,256]{3,1,0,2:T(8,128)S(1)} collective-permute-done((f32[4,16,8,256]{3,1,0,2:T(8,128)S(1)}, f32[4,16,8,256]{3,1,0,2:T(8,128)S(1)}, u32[]{:S(2)}, u32[]{:S(2)}) %collective-permute-start.12) | collective-permute-done | bytes 524320 | tf_op jit(solution)/shard_map/ppermute | solution.py:29
  217.9 1.5 collective-permute-done.11
  219.9 1.6 collective-permute-start.13
  221.6 9.3 %collective-permute-done.14 = f32[4,16,8,256]{3,1,0,2:T(8,128)S(1)} collective-permute-done((f32[4,16,8,256]{3,1,0,2:T(8,128)S(1)}, f32[4,16,8,256]{3,1,0,2:T(8,128)S(1)}, u32[]{:S(2)}, u32[]{:S(2)}) %collective-permute-start.14) | collective-permute-done | bytes 524320 | tf_op jit(solution)/shard_map/ppermute | solution.py:29
  233.0 1.6 collective-permute-start.15
  234.7 8.5 %collective-permute-done.16 = f32[4,16,8,256]{3,1,0,2:T(8,128)S(1)} collective-permute-done((f32[4,16,8,256]{3,1,0,2:T(8,128)S(1)}, f32[4,16,8,256]{3,1,0,2:T(8,128)S(1)}, u32[]{:S(2)}, u32[]{:S(2)}) %collective-permute-start.16) | collective-permute-done | bytes 524320 | tf_op jit(solution)/shard_map/ppermute | solution.py:29
  247.0 7.6 %collective-permute-done.18 = f32[4,16,8,256]{3,1,0,2:T(8,128)S(1)} collective-permute-done((f32[4,16,8,256]{3,1,0,2:T(8,128)S(1)}, f32[4,16,8,256]{3,1,0,2:T(8,128)S(1)}, u32[]{:S(2)}, u32[]{:S(2)}) %collective-permute-start.18) | collective-permute-done | bytes 524320 | tf_op jit(solution)/shard_map/ppermute | solution.py:29
  254.7 2.5 collective-permute-done.17
  257.5 2.1 collective-permute-start.20
  259.7 3.3 %collective-permute-done.20 = f32[16,8,256]{2,0,1:T(8,128)S(1)} collective-permute-done((f32[16,8,256]{2,0,1:T(8,128)S(1)}, f32[16,8,256]{2,0,1:T(8,128)S(1)}, u32[]{:S(2)}, u32[]{:S(2)}) %collective-permute-start.20) | collective-permute-done | bytes 131104 | tf_op jit(solution)/shard_map/ppermute | solution.py:29
  263.0 3.9 %collective-permute-done.19 = f32[16,8,256]{2,0,1:T(8,128)S(1)} collective-permute-done((f32[16,8,256]{2,0,1:T(8,128)S(1)}, f32[16,8,256]{2,0,1:T(8,128)S(1)}, u32[]{:S(2)}, u32[]{:S(2)}) %collective-permute-start.19) | collective-permute-done | bytes 131104 | tf_op jit(solution)/shard_map/ppermute | solution.py:28
  267.7 2.0 collective-permute-start.21
  269.7 2.5 collective-permute-done.22
  272.2 1.7 collective-permute-done.21
  274.8 2.4 collective-permute-start.24
  277.3 2.9 %collective-permute-done.23 = f32[16,8,256]{2,0,1:T(8,128)S(1)} collective-permute-done((f32[16,8,256]{2,0,1:T(8,128)S(1)}, f32[16,8,256]{2,0,1:T(8,128)S(1)}, u32[]{:S(2)}, u32[]{:S(2)}) %collective-permute-start.23) | collective-permute-done | bytes 131104 | tf_op jit(solution)/shard_map/ppermute | solution.py:28
  281.5 3.8 %fusion.55 = (f32[16,1,512]{2,0,1:T(8,128)S(1)}, f32[16,1,512]{2,0,1:T(8,128)S(1)}, f32[16,1,512]{2,0,1:T(8,128)S(1)}, f32[16,1,512]{2,0,1:T(8,128)S(1)}, f32[16...) fusion(f32[16,2,4,512]{3,0,2,1:T(8,128)S(1)} %bitcast.881, f32[512]{0:T(512)S(1)} %bitcast.889, ...), kind=kLoop, calls=%fused_computation.454 | loop fusion | flops 196608 | bytes 399494 | tf_op jit(solution)/shard_map/jit(_where)/select_n | solution.py:131
  (217 shorter events, 55.4 us)
Async XLA Ops:
  0.0 124.1 %collective-permute-start = (f32[1536,1024]{1,0:T(8,128)}, f32[1536,1024]{1,0:T(8,128)}, u32[]{:S(2)}, u32[]{:S(2)}) collective-permute-start(f32[1536,1024]{1,0:T(8,128)} %param.2), channel_id=1, source_target_pairs={{1,0},{2,1},{3,2},{4,3},{5,4},{6,5},{7,6},{9,8},{10,9},{11,10},{12... | collective-permute-start | bytes 18874376 | tf_op jit(solution)/shard_map/ppermute | solution.py:17
  64.7 59.3 %collective-permute-start.1 = (f32[2,1024]{1,0:T(2,128)}, f32[2,1024]{1,0:T(2,128)S(1)}, u32[]{:S(2)}, u32[]{:S(2)}) collective-permute-start(f32[2,1024]{1,0:T(2,128)} %pad_maximum_fusion.2), channel_id=1, source_target_pairs={{1,0},{2,1},{3,2},{4,3},{5,4},{6,5},{7,6},{9,8},{10,9},{11,10},{12... | collective-permute-start | bytes 24584 | tf_op jit(solution)/shard_map/ppermute | solution.py:17
  66.7 56.6 %collective-permute-start.4 = (f32[2,512]{1,0:T(2,128)S(1)}, f32[2,512]{1,0:T(2,128)}, u32[]{:S(2)}, u32[]{:S(2)}) collective-permute-start(f32[2,512]{1,0:T(2,128)S(1)} %fusion.68), channel_id=1, source_target_pairs={{2,0},{3,1},{4,2},{5,3},{6,4},{7,5},{10,8},{11,9},{12,10},{13,11},... | collective-permute-start | bytes 12296 | tf_op jit(solution)/shard_map/ppermute | solution.py:17
  72.4 77.7 %collective-permute-start.2 = (f32[1536,512]{1,0:T(8,128)}, f32[1536,512]{1,0:T(8,128)}, u32[]{:S(2)}, u32[]{:S(2)}) collective-permute-start(f32[1536,512]{1,0:T(8,128)} %slice.536), channel_id=1, source_target_pairs={{3,1},{5,3},{7,5},{11,9},{13,11},{15,13},{19,17},{21,19},{23,21},{... | collective-permute-start | bytes 9437192 | tf_op jit(solution)/shard_map/ppermute | solution.py:79
  117.6 10.2 %slice-start = ((s8[6291456]{0:T(1024)(128)(4,1)}), s8[2097152]{0:T(1024)(128)(4,1)S(1)}, s32[]{:S(2)}) async-start(s8[6291456]{0:T(1024)(128)(4,1)} %bitcast.870), calls=%async_computation | async-start | bytes 4194304
  124.1 4.0 %slice-start.1 = ((s8[6291456]{0:T(1024)(128)(4,1)}), s8[4194304]{0:T(1024)(128)(4,1)S(1)}, s32[]{:S(2)}) async-start(s8[6291456]{0:T(1024)(128)(4,1)} %bitcast.870), calls=%async_computation.1 | async-start | bytes 8388608
  138.8 11.4 %collective-permute-start.3 = (f32[1536,512]{1,0:T(8,128)S(1)}, f32[1536,512]{1,0:T(8,128)S(1)}, u32[]{:S(2)}, u32[]{:S(2)}) collective-permute-start(f32[1536,512]{1,0:T(8,128)S(1)} %slice.704), channel_id=1, source_target_pairs={{1,0},{3,2},{5,4},{7,6},{9,8},{11,10},{13,12},{15,14},{17,16},{19,... | collective-permute-start | bytes 9437192 | tf_op jit(solution)/shard_map/ppermute | solution.py:80
  140.5 1.0 copy-start.4
  140.5 1.2 copy-start.3
  141.8 1.0 copy-start.2
  141.8 1.2 copy-start.1
  141.8 1.3 copy-start
  141.8 1.5 copy-start.12
  141.8 1.6 copy-start.11
  142.4 1.3 copy-start.13
  142.4 1.5 copy-start.10
  142.4 1.6 copy-start.9
  142.4 1.8 copy-start.8
  142.4 1.9 copy-start.7
  142.5 2.1 copy-start.6
  142.5 2.2 copy-start.5
  156.9 14.2 %collective-permute-start.6 = (f32[4,16,8,256]{3,1,0,2:T(8,128)S(1)}, f32[4,16,8,256]{3,1,0,2:T(8,128)S(1)}, u32[]{:S(2)}, u32[]{:S(2)}) collective-permute-start(f32[4,16,8,256]{3,1,0,2:T(8,128)S(1)} %constant_dynamic-update-slice_fusion.8), channel_id=1, source_target_pairs={{0,56},{8,0},{16,8},{24,16},{32,24},{40,32},{48,40},{56,48},{1,57}... | collective-permute-start | bytes 1572872 | tf_op jit(solution)/shard_map/ppermute | solution.py:29
  158.9 16.1 %collective-permute-start.5 = (f32[4,16,8,256]{3,1,0,2:T(8,128)}, f32[4,16,8,256]{3,1,0,2:T(8,128)S(1)}, u32[]{:S(2)}, u32[]{:S(2)}) collective-permute-start(f32[4,16,8,256]{3,1,0,2:T(8,128)} %get-tuple-element.25), channel_id=1, source_target_pairs={{0,8},{8,16},{16,24},{24,32},{32,40},{40,48},{48,56},{56,0},{1,9},... | collective-permute-start | bytes 1572872 | tf_op jit(solution)/shard_map/ppermute | solution.py:28
  175.1 14.0 %collective-permute-start.8 = (f32[4,16,8,256]{3,1,0,2:T(8,128)S(1)}, f32[4,16,8,256]{3,1,0,2:T(8,128)S(1)}, u32[]{:S(2)}, u32[]{:S(2)}) collective-permute-start(f32[4,16,8,256]{3,1,0,2:T(8,128)S(1)} %add.603), channel_id=1, source_target_pairs={{0,56},{8,0},{16,8},{24,16},{32,24},{40,32},{48,40},{56,48},{1,57}... | collective-permute-start | bytes 1572872 | tf_op jit(solution)/shard_map/ppermute | solution.py:29
  175.2 15.2 %collective-permute-start.7 = (f32[4,16,8,256]{3,1,0,2:T(8,128)S(1)}, f32[4,16,8,256]{3,1,0,2:T(8,128)S(1)}, u32[]{:S(2)}, u32[]{:S(2)}) collective-permute-start(f32[4,16,8,256]{3,1,0,2:T(8,128)S(1)} %add.599), channel_id=1, source_target_pairs={{0,8},{8,16},{16,24},{24,32},{32,40},{40,48},{48,56},{56,0},{1,9},... | collective-permute-start | bytes 1572872 | tf_op jit(solution)/shard_map/ppermute | solution.py:28
  190.5 13.3 %collective-permute-start.10 = (f32[4,16,8,256]{3,1,0,2:T(8,128)S(1)}, f32[4,16,8,256]{3,1,0,2:T(8,128)S(1)}, u32[]{:S(2)}, u32[]{:S(2)}) collective-permute-start(f32[4,16,8,256]{3,1,0,2:T(8,128)S(1)} %add.611), channel_id=1, source_target_pairs={{0,56},{8,0},{16,8},{24,16},{32,24},{40,32},{48,40},{56,48},{1,57}... | collective-permute-start | bytes 1572872 | tf_op jit(solution)/shard_map/ppermute | solution.py:29
  191.1 14.3 %collective-permute-start.9 = (f32[4,16,8,256]{3,1,0,2:T(8,128)S(1)}, f32[4,16,8,256]{3,1,0,2:T(8,128)S(1)}, u32[]{:S(2)}, u32[]{:S(2)}) collective-permute-start(f32[4,16,8,256]{3,1,0,2:T(8,128)S(1)} %add.607), channel_id=1, source_target_pairs={{0,8},{8,16},{16,24},{24,32},{32,40},{40,48},{48,56},{56,0},{1,9},... | collective-permute-start | bytes 1572872 | tf_op jit(solution)/shard_map/ppermute | solution.py:28
  205.5 12.3 %collective-permute-start.12 = (f32[4,16,8,256]{3,1,0,2:T(8,128)S(1)}, f32[4,16,8,256]{3,1,0,2:T(8,128)S(1)}, u32[]{:S(2)}, u32[]{:S(2)}) collective-permute-start(f32[4,16,8,256]{3,1,0,2:T(8,128)S(1)} %add.619), channel_id=1, source_target_pairs={{0,56},{8,0},{16,8},{24,16},{32,24},{40,32},{48,40},{56,48},{1,57}... | collective-permute-start | bytes 1572872 | tf_op jit(solution)/shard_map/ppermute | solution.py:29
  205.9 13.4 %collective-permute-start.11 = (f32[4,16,8,256]{3,1,0,2:T(8,128)S(1)}, f32[4,16,8,256]{3,1,0,2:T(8,128)S(1)}, u32[]{:S(2)}, u32[]{:S(2)}) collective-permute-start(f32[4,16,8,256]{3,1,0,2:T(8,128)S(1)} %add.615), channel_id=1, source_target_pairs={{0,8},{8,16},{16,24},{24,32},{32,40},{40,48},{48,56},{56,0},{1,9},... | collective-permute-start | bytes 1572872 | tf_op jit(solution)/shard_map/ppermute | solution.py:28
  219.4 11.5 %collective-permute-start.14 = (f32[4,16,8,256]{3,1,0,2:T(8,128)S(1)}, f32[4,16,8,256]{3,1,0,2:T(8,128)S(1)}, u32[]{:S(2)}, u32[]{:S(2)}) collective-permute-start(f32[4,16,8,256]{3,1,0,2:T(8,128)S(1)} %add.627), channel_id=1, source_target_pairs={{0,56},{8,0},{16,8},{24,16},{32,24},{40,32},{48,40},{56,48},{1,57}... | collective-permute-start | bytes 1572872 | tf_op jit(solution)/shard_map/ppermute | solution.py:29
  219.9 12.6 %collective-permute-start.13 = (f32[4,16,8,256]{3,1,0,2:T(8,128)S(1)}, f32[4,16,8,256]{3,1,0,2:T(8,128)S(1)}, u32[]{:S(2)}, u32[]{:S(2)}) collective-permute-start(f32[4,16,8,256]{3,1,0,2:T(8,128)S(1)} %add.623), channel_id=1, source_target_pairs={{0,8},{8,16},{16,24},{24,32},{32,40},{40,48},{48,56},{56,0},{1,9},... | collective-permute-start | bytes 1572872 | tf_op jit(solution)/shard_map/ppermute | solution.py:28
  232.6 10.6 %collective-permute-start.16 = (f32[4,16,8,256]{3,1,0,2:T(8,128)S(1)}, f32[4,16,8,256]{3,1,0,2:T(8,128)S(1)}, u32[]{:S(2)}, u32[]{:S(2)}) collective-permute-start(f32[4,16,8,256]{3,1,0,2:T(8,128)S(1)} %add.635), channel_id=1, source_target_pairs={{0,56},{8,0},{16,8},{24,16},{32,24},{40,32},{48,40},{56,48},{1,57}... | collective-permute-start | bytes 1572872 | tf_op jit(solution)/shard_map/ppermute | solution.py:29
  233.0 11.7 %collective-permute-start.15 = (f32[4,16,8,256]{3,1,0,2:T(8,128)S(1)}, f32[4,16,8,256]{3,1,0,2:T(8,128)S(1)}, u32[]{:S(2)}, u32[]{:S(2)}) collective-permute-start(f32[4,16,8,256]{3,1,0,2:T(8,128)S(1)} %add.631), channel_id=1, source_target_pairs={{0,8},{8,16},{16,24},{24,32},{32,40},{40,48},{48,56},{56,0},{1,9},... | collective-permute-start | bytes 1572872 | tf_op jit(solution)/shard_map/ppermute | solution.py:28
  244.8 14.7 %copy-start.14 = (s32[2]{0:T(128)S(1)}, s32[2]{0:T(128)}, u32[]{:S(2)}) copy-start(s32[2]{0:T(128)} %param.3) | copy-start | bytes 28
  244.9 9.7 %collective-permute-start.18 = (f32[4,16,8,256]{3,1,0,2:T(8,128)S(1)}, f32[4,16,8,256]{3,1,0,2:T(8,128)S(1)}, u32[]{:S(2)}, u32[]{:S(2)}) collective-permute-start(f32[4,16,8,256]{3,1,0,2:T(8,128)S(1)} %add.640), channel_id=1, source_target_pairs={{0,56},{8,0},{16,8},{24,16},{32,24},{40,32},{48,40},{56,48},{1,57}... | collective-permute-start | bytes 1572872 | tf_op jit(solution)/shard_map/ppermute | solution.py:29
  246.4 10.9 %collective-permute-start.17 = (f32[4,16,8,256]{3,1,0,2:T(8,128)S(1)}, f32[4,16,8,256]{3,1,0,2:T(8,128)S(1)}, u32[]{:S(2)}, u32[]{:S(2)}) collective-permute-start(f32[4,16,8,256]{3,1,0,2:T(8,128)S(1)} %add.639), channel_id=1, source_target_pairs={{0,8},{8,16},{16,24},{24,32},{32,40},{40,48},{48,56},{56,0},{1,9},... | collective-permute-start | bytes 1572872 | tf_op jit(solution)/shard_map/ppermute | solution.py:28
  257.5 5.5 %collective-permute-start.20 = (f32[16,8,256]{2,0,1:T(8,128)S(1)}, f32[16,8,256]{2,0,1:T(8,128)S(1)}, u32[]{:S(2)}, u32[]{:S(2)}) collective-permute-start(f32[16,8,256]{2,0,1:T(8,128)S(1)} %slice.830), channel_id=1, source_target_pairs={{0,192},{64,0},{128,64},{192,128},{1,193},{65,1},{129,65},{193,129... | collective-permute-start | bytes 393224 | tf_op jit(solution)/shard_map/ppermute | solution.py:29
  259.6 7.2 %collective-permute-start.19 = (f32[16,8,256]{2,0,1:T(8,128)S(1)}, f32[16,8,256]{2,0,1:T(8,128)S(1)}, u32[]{:S(2)}, u32[]{:S(2)}) collective-permute-start(f32[16,8,256]{2,0,1:T(8,128)S(1)} %slice.829), channel_id=1, source_target_pairs={{0,64},{64,128},{128,192},{192,0},{1,65},{65,129},{129,193},{193,1... | collective-permute-start | bytes 393224 | tf_op jit(solution)/shard_map/ppermute | solution.py:28
  266.9 5.3 %collective-permute-start.22 = (f32[16,8,256]{2,0,1:T(8,128)S(1)}, f32[16,8,256]{2,0,1:T(8,128)S(1)}, u32[]{:S(2)}, u32[]{:S(2)}) collective-permute-start(f32[16,8,256]{2,0,1:T(8,128)S(1)} %slice_add_fusion.4), channel_id=1, source_target_pairs={{0,192},{64,0},{128,64},{192,128},{1,193},{65,1},{129,65},{193,129... | collective-permute-start | bytes 393224 | tf_op jit(solution)/shard_map/ppermute | solution.py:29
  267.7 6.2 %collective-permute-start.21 = (f32[16,8,256]{2,0,1:T(8,128)S(1)}, f32[16,8,256]{2,0,1:T(8,128)S(1)}, u32[]{:S(2)}, u32[]{:S(2)}) collective-permute-start(f32[16,8,256]{2,0,1:T(8,128)S(1)} %slice_add_fusion.5), channel_id=1, source_target_pairs={{0,64},{64,128},{128,192},{192,0},{1,65},{65,129},{129,193},{193,1... | collective-permute-start | bytes 393224 | tf_op jit(solution)/shard_map/ppermute | solution.py:28
  273.9 6.3 %collective-permute-start.23 = (f32[16,8,256]{2,0,1:T(8,128)S(1)}, f32[16,8,256]{2,0,1:T(8,128)S(1)}, u32[]{:S(2)}, u32[]{:S(2)}) collective-permute-start(f32[16,8,256]{2,0,1:T(8,128)S(1)} %slice_add_fusion.3), channel_id=1, source_target_pairs={{0,64},{64,128},{128,192},{192,0},{1,65},{65,129},{129,193},{193,1... | collective-permute-start | bytes 393224 | tf_op jit(solution)/shard_map/ppermute | solution.py:28
  274.8 5.4 %collective-permute-start.24 = (f32[16,8,256]{2,0,1:T(8,128)S(1)}, f32[16,8,256]{2,0,1:T(8,128)S(1)}, u32[]{:S(2)}, u32[]{:S(2)}) collective-permute-start(f32[16,8,256]{2,0,1:T(8,128)S(1)} %slice_add_fusion.2), channel_id=1, source_target_pairs={{0,192},{64,0},{128,64},{192,128},{1,193},{65,1},{129,65},{193,129... | collective-permute-start | bytes 393224 | tf_op jit(solution)/shard_map/ppermute | solution.py:29
where the time goes:
time: 292 us; the launch traced here: 287 us
  waiting for transfers between devices  97.3 us (33%)
  blocking collectives  52.4 us (18%)
  local copies, waits for them, and re-layouts  48.8 us (17%)
  matrix products  32.5 us (11%)
  starting transfers between devices  32.2 us (11%)
  other arithmetic  21.8 us (7%)
    ppermute x10, waiting for transfers between devices, ring_steps(): down = lax.ppermute(down, axis, backward) + piece_of(me + step + 2, 1)  76.3 us
    psum x4, blocking collectives, samp_sum(): return lax.psum(lax.psum(value, 'samp_z'), 'samp_x')  52.4 us
    unnamed x139, local copies, waits for them, and re-layouts  36.2 us
    dot_general x8, matrix products, tile(): lax.dot_general(left_panel, right_panel, transposed_dims, precision=HIGHE...  32.5 us
    ppermute x10, waiting for transfers between devices, ring_steps(): lax.ppermute(up, axis, forward) + piece_of(me - step - 2 + 2 * count, 0)  21 us
    ppermute x10, starting transfers between devices, ring_steps(): lax.ppermute(up, axis, forward) + piece_of(me - step - 2 + 2 * count, 0)  12.2 us
    ppermute x10, starting transfers between devices, ring_steps(): down = lax.ppermute(down, axis, backward) + piece_of(me + step + 2, 1)  10.1 us
    reduce_sum x1, other arithmetic, on_device(): square_sum = samp_sum(jnp.sum(deviation * deviation, axis=0))  6.63 us
  transfers between devices with their start and end apart: 25, of which 19 were waited for; matrix products, arithmetic and copies ran while one was open for 30% of the time, Pallas kernels for 0%

commit v1 on v0

--- a/solution.py
+++ b/solution.py
@@ -17,38 +17,72 @@
     return lax.ppermute(value, axis, [(source, source + steps) for source in range(first, last)])
 
 
-def ring_steps(piece_of, axis, count):
-    me = lax.axis_index(axis)
-    forward = [(i, (i + 1) % count) for i in range(count)]
-    backward = [(i, (i - 1) % count) for i in range(count)]
-    up = piece_of(me - 1 + count, 0)
-    down = piece_of(me + 1, 1)
-    for step in range(count - 1):
-        up, down = lax.optimization_barrier((up, down))
-        up = lax.ppermute(up, axis, forward) + piece_of(me - step - 2 + 2 * count, 0)
-        down = lax.ppermute(down, axis, backward) + piece_of(me + step + 2, 1)
-    return jnp.concatenate([up, down], axis=-1)
+class Ring:
+    def __init__(self, piece_of, axis, count):
+        self.piece_of, self.axis, self.count = piece_of, axis, count
+        self.me = lax.axis_index(axis)
+        self.state = (piece_of(self.me - 1 + count, 0), piece_of(self.me + 1, 1))
+        self.step = 0
+
+    def advance(self):
+        count, me = self.count, self.me
+        up, down = self.state
+        forward = [(i, (i + 1) % count) for i in range(count)]
+        backward = [(i, (i - 1) % count) for i in range(count)]
+        up = lax.ppermute(up, self.axis, forward) + self.piece_of(me - self.step - 2 + 2 * count, 0)
+        down = lax.ppermute(down, self.axis, backward) + self.piece_of(me + self.step + 2, 1)
+        self.state = (up, down)
+        self.step += 1
+
+    def done(self):
+        return self.step == self.count - 1
+
+    def result(self):
+        return jnp.concatenate(self.state, axis=-1)
+
+
+def run_together(rings):
+    while not all(ring.done() for ring in rings):
+        live = [ring for ring in rings if not ring.done()]
+        states = lax.optimization_barrier(tuple(ring.state for ring in live))
+        for ring, state in zip(live, states):
+            ring.state = state
+            ring.advance()
+    return [ring.result() for ring in rings]
+
+
+def sliced(piece, part, width):
+    return piece[..., part * width : (part + 1) * width]
 
 
 def ring_reduce_scatter(tiles, major, minor):
     major_count = lax.axis_size(major)
     minor_count = lax.axis_size(minor)
     rows = tiles[0].shape[0] // (major_count * minor_count)
-    half = tiles[0].shape[-1] // 2
+    quarter = tiles[0].shape[-1] // 4
     grouped = [t.reshape((major_count, minor_count, rows) + t.shape[1:]) for t in tiles]
 
-    def first_piece(index, part):
-        pieces = [lax.dynamic_index_in_dim(g, index % minor_count, 1, keepdims=False) for g in grouped]
-        pieces = [p[..., :half] if part == 0 else p[..., half:] for p in pieces]
-        return jnp.stack(pieces, axis=2)
+    def first_piece(axis_of_chunk, offset, count):
+        def piece_of(index, part):
+            pieces = [lax.dynamic_index_in_dim(g, index % count, axis_of_chunk, keepdims=False) for g in grouped]
+            return jnp.stack([sliced(p, offset + part, quarter) for p in pieces], axis=2)
 
-    partial = ring_steps(first_piece, minor, minor_count)
+        return piece_of
 
-    def second_piece(index, part):
-        piece = lax.dynamic_index_in_dim(partial, index % major_count, 0, keepdims=False)
-        return piece[..., :half] if part == 0 else piece[..., half:]
+    def second_piece(partial, count):
+        def piece_of(index, part):
+            piece = lax.dynamic_index_in_dim(partial, index % count, 0, keepdims=False)
+            return sliced(piece, part, quarter)
 
-    return ring_steps(second_piece, major, major_count)
+        return piece_of
+
+    early = run_together(
+        [Ring(first_piece(1, 0, minor_count), minor, minor_count), Ring(first_piece(0, 2, major_count), major, major_count)]
+    )
+    late = run_together(
+        [Ring(second_piece(early[0], major_count), major, major_count), Ring(second_piece(early[1], minor_count), minor, minor_count)]
+    )
+    return jnp.concatenate(late, axis=-1)
 
 
 def samp_size():

time: 292 us -> 298 us (1.021)
  starting transfers between devices: 32.2 us -> 77.7 us
  waiting for transfers between devices: 97.3 us -> 64.1 us
  matrix products: 32.5 us -> 27.9 us
    ppermute x20 -> x40, starting transfers between devices: 22.3 us -> 67.6 us  [the longest x20 46.7 us: advance(): lax.ppermute(down, self.axis, backward)]
    ppermute x20 -> x40, waiting for transfers between devices: 97.3 us -> 62.1 us  [the longest x20 53.3 us: advance(): lax.ppermute(up, self.axis, forward)]
    unnamed x139 -> x186, local copies, waits for them, and re-layouts: 36.2 us -> 28.3 us
    squeeze x4 -> x8, local copies, waits for them, and re-layouts: 3.39 us -> 8.12 us  [piece_of(): lax.dynamic_index_in_dim(g, index % count, axis_of_chunk, keepdims=False)]
    dot_general x8, matrix products: 32.5 us -> 27.9 us  [tile(): lax.dot_general(left_panel, right_panel, transposed_dims, precision=HIGHE...]
  transfers between devices with their start and end apart: 25 -> 45, of which waited for: 19 -> 24; matrix products, arithmetic and copies ran while one was open for 30% -> 28% of each run, Pallas kernels for 0% -> 0%
where the time goes in v1:
time: 298 us; the launch traced here: 293 us
  starting transfers between devices  77.7 us (26%)
  waiting for transfers between devices  64.1 us (22%)
  blocking collectives  52.4 us (18%)
  local copies, waits for them, and re-layouts  46.3 us (16%)
  matrix products  27.9 us (9%)
  other arithmetic  22.7 us (8%)
    ppermute x20, waiting for transfers between devices, advance(): lax.ppermute(up, self.axis, forward)  53.3 us
    psum x4, blocking collectives, samp_sum(): return lax.psum(lax.psum(value, 'samp_z'), 'samp_x')  52.4 us
    ppermute x20, starting transfers between devices, advance(): lax.ppermute(down, self.axis, backward)  46.7 us
    unnamed x186, local copies, waits for them, and re-layouts  28.3 us
    dot_general x8, matrix products, tile(): lax.dot_general(left_panel, right_panel, transposed_dims, precision=HIGHE...  27.9 us
    ppermute x20, starting transfers between devices, advance(): lax.ppermute(up, self.axis, forward)  20.9 us
    ppermute x20, waiting for transfers between devices, advance(): lax.ppermute(down, self.axis, backward)  8.72 us
    squeeze x8, local copies, waits for them, and re-layouts, piece_of(): lax.dynamic_index_in_dim(g, index % count, axis_of_chunk, keepdims=False)  8.12 us
  transfers between devices with their start and end apart: 45, of which 24 were waited for; matrix products, arithmetic and copies ran while one was open for 28% of the time, Pallas kernels for 0%

profile of v1, /device:TPU:8, one launch (start us, length us, event | category | flops | bytes accessed | tf_op | source)
XLA Modules:
  0.0 293.2 jit_solution(3037741669693915676)
XLA Ops:
  1.9 3.8 %slice.776 = f32[1536,512]{1,0:T(8,128)} slice(f32[1536,1024]{1,0:T(8,128)} %param.2), slice={[0:1536], [0:512]} | slice | bytes 6291456 | tf_op jit(solution)/shard_map/slice | solution.py:113
  5.7 2.3 collective-permute-start.2
  8.0 3.2 %reduce_sum.18 = f32[1024]{0:T(1024)S(1)} reduce(f32[1536,1024]{1,0:T(8,128)} %param.2, f32[]{:T(128)} %constant.996.clone.1), dimensions={0}, to_apply=%region_0.0 | reduce | flops 1571840 | bytes 6295556 | tf_op jit(solution)/shard_map/reduce_sum | solution.py:117
  11.2 20.0 %psum.28 = f32[1024]{0:T(1024)S(1)} all-reduce(f32[1024]{0:T(1024)S(1)} %reduce_sum.18), channel_id=1, replica_groups=mesh['samp_x'=4,'samp_z'=8,'snp'=8] {'samp_z'}, use_global_device_ids=true, to_apply=%region_1.0 | all-reduce | flops 1024 | bytes 8192 | tf_op jit(solution)/shard_map/psum | solution.py:93
  31.2 10.5 %psum.29 = f32[1024]{0:T(1024)S(1)} all-reduce(f32[1024]{0:T(1024)S(1)} %psum.28), channel_id=1, replica_groups=mesh['samp_x'=4,'samp_z'=8,'snp'=8] {'samp_x'}, use_global_device_ids=true, to_apply=%region_2.0 | all-reduce | flops 1024 | bytes 8192 | tf_op jit(solution)/shard_map/psum | solution.py:93
  41.7 6.7 %multiply_reduce_fusion = (f32[1024]{0:T(1024)S(1)}, f32[1536,1024]{1,0:T(8,128)}) fusion(f32[1536,1024]{1,0:T(8,128)} %param.2, f32[1024]{0:T(1024)S(1)} %broadcast_multiply_fusion), kind=kLoop, calls=%fused_computation | loop fusion | flops 4717568 | bytes 12591104 | tf_op jit(solution)/shard_map/reduce_sum | solution.py:120
  48.4 14.1 %psum.30 = f32[1024]{0:T(1024)S(1)} all-reduce(f32[1024]{0:T(1024)S(1)} %get-tuple-element.85), channel_id=1, replica_groups=mesh['samp_x'=4,'samp_z'=8,'snp'=8] {'samp_z'}, use_global_device_ids=true, to_apply=%region_4.0 | all-reduce | flops 1024 | bytes 8192 | tf_op jit(solution)/shard_map/psum | solution.py:93
  62.5 7.7 %psum.31 = f32[1024]{0:T(1024)S(1)} all-reduce(f32[1024]{0:T(1024)S(1)} %psum.30), channel_id=1, replica_groups=mesh['samp_x'=4,'samp_z'=8,'snp'=8] {'samp_x'}, use_global_device_ids=true, to_apply=%region_5.0 | all-reduce | flops 1024 | bytes 8192 | tf_op jit(solution)/shard_map/psum | solution.py:93
  72.8 2.4 collective-permute-start.1
  75.5 5.6 %fusion.13 = f32[512,512]{1,0:T(8,128)S(1)} fusion(f32[1536,1024]{1,0:T(8,128)} %get-tuple-element.86), kind=kOutput, calls=%fused_computation.44 | convolution fusion | flops 2415919104 | bytes 7340032 | tf_op jit(solution)/shard_map/dot_general | solution.py:139
  81.2 3.8 %fusion.15 = f32[512,512]{1,0:T(8,128)} fusion(f32[1536,1024]{1,0:T(8,128)S(1)} %copy-done), kind=kOutput, calls=%fused_computation.46 | convolution fusion | flops 2415919104 | bytes 4194304 | tf_op jit(solution)/shard_map/dot_general | solution.py:139
  85.0 3.0 %dynamic-slice_bitcast_fusion.54 = (f32[4,16,512]{2,1,0:T(8,128)S(1)}, f32[4,16,512]{2,1,0:T(8,128)}, f32[4,16,512]{2,1,0:T(8,128)}, f32[4,16,512]{2,1,0:T(8,128...) fusion(f32[4,8,16,512]{3,2,1,0:T(8,128)S(1)} %bitcast.1266, ...), kind=kLoop, calls=%fused_computation.359 | loop fusion | bytes 7340088 | tf_op jit(solution)/shard_map/jit(dynamic_index_in_dim)/squeeze | solution.py:67
  111.3 2.6 fusion.20
  114.8 3.5 %broadcast_subtract_fusion = f32[1536,1024]{1,0:T(8,128)S(1)} fusion(f32[1536,1024]{1,0:T(8,128)} %collective-permute-done, f32[1024]{0:T(1024)S(1)} %bitcast.1288), kind=kLoop, calls=%fused_computation.32 | loop fusion | flops 1572864 | bytes 12587008 | tf_op jit(solution)/shard_map/sub | solution.py:131
  118.3 3.0 %fusion.7 = f32[512,512]{1,0:T(8,128)S(1)} fusion(f32[1536,1024]{1,0:T(8,128)S(1)} %broadcast_subtract_fusion, f32[1536,1024]{1,0:T(8,128)S(1)} %bitcast.1265), kind=kOutput, calls=%fused_computation.38 | convolution fusion | flops 2415919104 | bytes 7340032 | tf_op jit(solution)/shard_map/dot_general | solution.py:139
  121.2 2.8 fusion.5
  124.0 2.8 fusion.9
  134.1 2.3 slice.1024
  139.1 2.8 fusion.3
  143.9 4.6 %fusion = f32[512,512]{1,0:T(8,128)S(1)} fusion(f32[1536,512]{1,0:T(8,128)} %collective-permute-done.2, f32[1536,512]{1,0:T(8,128)S(1)} %collective-permute-done.3, f32[1536,1024]{1,0:T(8,128)S(1)} %bitcast.1265, f32[512]{0:T(512)S(1)} %bitcast.1292), kind=kOutput, calls=%fused_computation.29 | convolution fusion | flops 2417491968 | bytes 10487808 | tf_op jit(solution)/shard_map/dot_general | solution.py:139
  152.2 2.1 collective-permute-start.5
  159.1 2.8 collective-permute-done.5
  162.4 7.7 %collective-permute-done.7 = f32[8,16,8,128]{3,1,0,2:T(8,128)S(1)} collective-permute-done((f32[8,16,8,128]{3,1,0,2:T(8,128)S(1)}, f32[8,16,8,128]{3,1,0,2:T(8,128)S(1)}, u32[]{:S(2)}, u32[]{:S(2)}) %collective-permute-start.7) | collective-permute-done | bytes 524320 | tf_op jit(solution)/shard_map/ppermute | solution.py:32
  171.2 3.3 %collective-permute-start.12 = (f32[8,16,8,128]{3,1,0,2:T(8,128)S(1)}, f32[8,16,8,128]{3,1,0,2:T(8,128)S(1)}, u32[]{:S(2)}, u32[]{:S(2)}) collective-permute-start(f32[8,16,8,128]{3,1,0,2:T(8,128)S(1)} %add.871), channel_id=1, source_target_pairs={{0,192},{64,0},{128,64},{192,128},{1,193},{65,1},{129,65},{193,129... | collective-permute-start | bytes 1572872 | tf_op jit(solution)/shard_map/ppermute | solution.py:33
  175.3 2.4 collective-permute-start.10
  177.8 4.3 %collective-permute-done.9 = f32[4,16,8,128]{3,1,0,2:T(8,128)S(1)} collective-permute-done((f32[4,16,8,128]{3,1,0,2:T(8,128)S(1)}, f32[4,16,8,128]{3,1,0,2:T(8,128)S(1)}, u32[]{:S(2)}, u32[]{:S(2)}) %collective-permute-start.9) | collective-permute-done | bytes 262176 | tf_op jit(solution)/shard_map/ppermute | solution.py:32
  182.2 2.1 collective-permute-done.11
  185.3 2.4 collective-permute-start.14
  187.8 4.3 %collective-permute-done.13 = f32[4,16,8,128]{3,1,0,2:T(8,128)S(1)} collective-permute-done((f32[4,16,8,128]{3,1,0,2:T(8,128)S(1)}, f32[4,16,8,128]{3,1,0,2:T(8,128)S(1)}, u32[]{:S(2)}, u32[]{:S(2)}) %collective-permute-start.13) | collective-permute-done | bytes 262176 | tf_op jit(solution)/shard_map/ppermute | solution.py:32
  192.5 3.1 %collective-permute-start.16 = (f32[4,16,8,128]{3,1,0,2:T(8,128)S(1)}, f32[4,16,8,128]{3,1,0,2:T(8,128)S(1)}, u32[]{:S(2)}, u32[]{:S(2)}) collective-permute-start(f32[4,16,8,128]{3,1,0,2:T(8,128)S(1)} %add.892), channel_id=1, source_target_pairs={{0,56},{8,0},{16,8},{24,16},{32,24},{40,32},{48,40},{56,48},{1,57}... | collective-permute-start | bytes 786440 | tf_op jit(solution)/shard_map/ppermute | solution.py:33
  195.6 3.4 %collective-permute-start.24 = (f32[8,16,8,128]{3,1,0,2:T(8,128)S(1)}, f32[8,16,8,128]{3,1,0,2:T(8,128)S(1)}, u32[]{:S(2)}, u32[]{:S(2)}) collective-permute-start(f32[8,16,8,128]{3,1,0,2:T(8,128)S(1)} %add.884), channel_id=1, source_target_pairs={{0,192},{64,0},{128,64},{192,128},{1,193},{65,1},{129,65},{193,129... | collective-permute-start | bytes 1572872 | tf_op jit(solution)/shard_map/ppermute | solution.py:33
  204.4 5.8 %collective-permute-done.17 = f32[4,16,8,128]{3,1,0,2:T(8,128)S(1)} collective-permute-done((f32[4,16,8,128]{3,1,0,2:T(8,128)S(1)}, f32[4,16,8,128]{3,1,0,2:T(8,128)S(1)}, u32[]{:S(2)}, u32[]{:S(2)}) %collective-permute-start.17) | collective-permute-done | bytes 262176 | tf_op jit(solution)/shard_map/ppermute | solution.py:32
  211.6 2.4 collective-permute-start.19
  214.9 6.6 %collective-permute-done.19 = f32[4,16,8,128]{3,1,0,2:T(8,128)S(1)} collective-permute-done((f32[4,16,8,128]{3,1,0,2:T(8,128)S(1)}, f32[4,16,8,128]{3,1,0,2:T(8,128)S(1)}, u32[]{:S(2)}, u32[]{:S(2)}) %collective-permute-start.19) | collective-permute-done | bytes 262176 | tf_op jit(solution)/shard_map/ppermute | solution.py:32
  223.2 2.2 collective-permute-start.22
  225.6 4.0 %collective-permute-done.22 = f32[4,16,8,128]{3,1,0,2:T(8,128)S(1)} collective-permute-done((f32[4,16,8,128]{3,1,0,2:T(8,128)S(1)}, f32[4,16,8,128]{3,1,0,2:T(8,128)S(1)}, u32[]{:S(2)}, u32[]{:S(2)}) %collective-permute-start.22) | collective-permute-done | bytes 262176 | tf_op jit(solution)/shard_map/ppermute | solution.py:33
  233.7 2.8 collective-permute-start.26
  237.8 2.3 collective-permute-start.28
  240.2 2.2 collective-permute-done.27
  242.4 2.1 collective-permute-start.30
  261.0 2.3 collective-permute-done.37
  266.8 2.2 collective-permute-done.39
  269.2 3.1 %collective-permute-start.42 = (f32[16,8,128]{2,0,1:T(8,128)S(1)}, f32[16,8,128]{2,0,1:T(8,128)S(1)}, u32[]{:S(2)}, u32[]{:S(2)}) collective-permute-start(f32[16,8,128]{2,0,1:T(8,128)S(1)} %slice_add_fusion.4), channel_id=1, source_target_pairs={{0,56},{8,0},{16,8},{24,16},{32,24},{40,32},{48,40},{56,48},{1,57}... | collective-permute-start | bytes 196616 | tf_op jit(solution)/shard_map/ppermute | solution.py:33
  272.3 3.4 %collective-permute-start.34 = (f32[16,8,128]{2,0,1:T(8,128)S(1)}, f32[16,8,128]{2,0,1:T(8,128)S(1)}, u32[]{:S(2)}, u32[]{:S(2)}) collective-permute-start(f32[16,8,128]{2,0,1:T(8,128)S(1)} %slice_add_fusion.14), channel_id=1, source_target_pairs={{0,192},{64,0},{128,64},{192,128},{1,193},{65,1},{129,65},{193,129... | collective-permute-start | bytes 196616 | tf_op jit(solution)/shard_map/ppermute | solution.py:33
  275.8 5.5 %collective-permute-done.41 = f32[16,8,128]{2,0,1:T(8,128)S(1)} collective-permute-done((f32[16,8,128]{2,0,1:T(8,128)S(1)}, f32[16,8,128]{2,0,1:T(8,128)S(1)}, u32[]{:S(2)}, u32[]{:S(2)}) %collective-permute-start.41) | collective-permute-done | bytes 65568 | tf_op jit(solution)/shard_map/ppermute | solution.py:32
  281.3 3.2 %collective-permute-start.44 = (f32[16,8,128]{2,0,1:T(8,128)S(1)}, f32[16,8,128]{2,0,1:T(8,128)S(1)}, u32[]{:S(2)}, u32[]{:S(2)}) collective-permute-start(f32[16,8,128]{2,0,1:T(8,128)S(1)} %slice_add_fusion.2), channel_id=1, source_target_pairs={{0,56},{8,0},{16,8},{24,16},{32,24},{40,32},{48,40},{56,48},{1,57}... | collective-permute-start | bytes 196616 | tf_op jit(solution)/shard_map/ppermute | solution.py:33
  284.6 2.2 collective-permute-done.43
  288.2 3.8 %fusion.83 = (f32[16,1,512]{2,0,1:T(8,128)S(1)}, f32[16,1,512]{2,0,1:T(8,128)S(1)}, f32[16,1,512]{2,0,1:T(8,128)S(1)}, f32[16,1,512]{2,0,1:T(8,128)S(1)}, f32[16...) fusion(f32[16,2,4,512]{3,0,2,1:T(8,128)S(1)} %bitcast.1283, f32[512]{0:T(512)S(1)} %bitcast.1291, ...), kind=kLoop, calls=%fused_computation.573 | loop fusion | flops 196608 | bytes 399494 | tf_op jit(solution)/shard_map/jit(_where)/select_n | solution.py:165
  (338 shorter events, 89.4 us)
Async XLA Ops:
  0.0 114.8 %collective-permute-start = (f32[1536,1024]{1,0:T(8,128)}, f32[1536,1024]{1,0:T(8,128)}, u32[]{:S(2)}, u32[]{:S(2)}) collective-permute-start(f32[1536,1024]{1,0:T(8,128)} %param.2), channel_id=1, source_target_pairs={{1,0},{2,1},{3,2},{4,3},{5,4},{6,5},{7,6},{9,8},{10,9},{11,10},{12... | collective-permute-start | bytes 18874376 | tf_op jit(solution)/shard_map/ppermute | solution.py:17
  5.7 136.1 %collective-permute-start.2 = (f32[1536,512]{1,0:T(8,128)}, f32[1536,512]{1,0:T(8,128)}, u32[]{:S(2)}, u32[]{:S(2)}) collective-permute-start(f32[1536,512]{1,0:T(8,128)} %slice.776), channel_id=1, source_target_pairs={{3,1},{5,3},{7,5},{11,9},{13,11},{15,13},{19,17},{21,19},{23,21},{... | collective-permute-start | bytes 9437192 | tf_op jit(solution)/shard_map/ppermute | solution.py:113
  70.3 43.7 %collective-permute-start.4 = (f32[2,512]{1,0:T(2,128)S(1)}, f32[2,512]{1,0:T(2,128)}, u32[]{:S(2)}, u32[]{:S(2)}) collective-permute-start(f32[2,512]{1,0:T(2,128)S(1)} %fusion.96), channel_id=1, source_target_pairs={{2,0},{3,1},{4,2},{5,3},{6,4},{7,5},{10,8},{11,9},{12,10},{13,11},... | collective-permute-start | bytes 12296 | tf_op jit(solution)/shard_map/ppermute | solution.py:17
  72.8 41.9 %collective-permute-start.1 = (f32[2,1024]{1,0:T(2,128)}, f32[2,1024]{1,0:T(2,128)S(1)}, u32[]{:S(2)}, u32[]{:S(2)}) collective-permute-start(f32[2,1024]{1,0:T(2,128)} %pad_maximum_fusion.2), channel_id=1, source_target_pairs={{1,0},{2,1},{3,2},{4,3},{5,4},{6,5},{7,6},{9,8},{10,9},{11,10},{12... | collective-permute-start | bytes 24584 | tf_op jit(solution)/shard_map/ppermute | solution.py:17
  85.0 26.3 %slice-start = ((s8[6291456]{0:T(1024)(128)(4,1)}), s8[2097152]{0:T(1024)(128)(4,1)S(1)}, s32[]{:S(2)}) async-start(s8[6291456]{0:T(1024)(128)(4,1)} %bitcast.1264), calls=%async_computation | async-start | bytes 4194304
  102.6 8.7 %slice-start.1 = ((s8[6291456]{0:T(1024)(128)(4,1)}), s8[4194304]{0:T(1024)(128)(4,1)S(1)}, s32[]{:S(2)}) async-start(s8[6291456]{0:T(1024)(128)(4,1)} %bitcast.1264), calls=%async_computation.1 | async-start | bytes 8388608
  136.3 7.6 %collective-permute-start.3 = (f32[1536,512]{1,0:T(8,128)S(1)}, f32[1536,512]{1,0:T(8,128)S(1)}, u32[]{:S(2)}, u32[]{:S(2)}) collective-permute-start(f32[1536,512]{1,0:T(8,128)S(1)} %slice.1024), channel_id=1, source_target_pairs={{1,0},{3,2},{5,4},{7,6},{9,8},{11,10},{13,12},{15,14},{17,16},{19,... | collective-permute-start | bytes 9437192 | tf_op jit(solution)/shard_map/ppermute | solution.py:114
  152.2 9.6 %collective-permute-start.5 = (f32[4,16,8,128]{3,1,0,2:T(8,128)S(1)}, f32[4,16,8,128]{3,1,0,2:T(8,128)S(1)}, u32[]{:S(2)}, u32[]{:S(2)}) collective-permute-start(f32[4,16,8,128]{3,1,0,2:T(8,128)S(1)} %get-tuple-element.45), channel_id=1, source_target_pairs={{0,8},{8,16},{16,24},{24,32},{32,40},{40,48},{48,56},{56,0},{1,9},... | collective-permute-start | bytes 786440 | tf_op jit(solution)/shard_map/ppermute | solution.py:32
  154.3 8.1 %collective-permute-start.6 = (f32[4,16,8,128]{3,1,0,2:T(8,128)S(1)}, f32[4,16,8,128]{3,1,0,2:T(8,128)S(1)}, u32[]{:S(2)}, u32[]{:S(2)}) collective-permute-start(f32[4,16,8,128]{3,1,0,2:T(8,128)S(1)} %constant_dynamic-update-slice_fusion.8), channel_id=1, source_target_pairs={{0,56},{8,0},{16,8},{24,16},{32,24},{40,32},{48,40},{56,48},{1,57}... | collective-permute-start | bytes 786440 | tf_op jit(solution)/shard_map/ppermute | solution.py:33
  155.5 14.6 %collective-permute-start.7 = (f32[8,16,8,128]{3,1,0,2:T(8,128)S(1)}, f32[8,16,8,128]{3,1,0,2:T(8,128)S(1)}, u32[]{:S(2)}, u32[]{:S(2)}) collective-permute-start(f32[8,16,8,128]{3,1,0,2:T(8,128)S(1)} %get-tuple-element.47), channel_id=1, source_target_pairs={{0,64},{64,128},{128,192},{192,0},{1,65},{65,129},{129,193},{193,1... | collective-permute-start | bytes 1572872 | tf_op jit(solution)/shard_map/ppermute | solution.py:32
  157.5 13.1 %collective-permute-start.8 = (f32[8,16,8,128]{3,1,0,2:T(8,128)S(1)}, f32[8,16,8,128]{3,1,0,2:T(8,128)S(1)}, u32[]{:S(2)}, u32[]{:S(2)}) collective-permute-start(f32[8,16,8,128]{3,1,0,2:T(8,128)S(1)} %constant_dynamic-update-slice_fusion.24), channel_id=1, source_target_pairs={{0,192},{64,0},{128,64},{192,128},{1,193},{65,1},{129,65},{193,129... | collective-permute-start | bytes 1572872 | tf_op jit(solution)/shard_map/ppermute | solution.py:33
  170.7 13.6 %collective-permute-start.11 = (f32[8,16,8,128]{3,1,0,2:T(8,128)S(1)}, f32[8,16,8,128]{3,1,0,2:T(8,128)S(1)}, u32[]{:S(2)}, u32[]{:S(2)}) collective-permute-start(f32[8,16,8,128]{3,1,0,2:T(8,128)S(1)} %add.867), channel_id=1, source_target_pairs={{0,64},{64,128},{128,192},{192,0},{1,65},{65,129},{129,193},{193,1... | collective-permute-start | bytes 1572872 | tf_op jit(solution)/shard_map/ppermute | solution.py:32
  171.2 13.2 %collective-permute-start.12 = (f32[8,16,8,128]{3,1,0,2:T(8,128)S(1)}, f32[8,16,8,128]{3,1,0,2:T(8,128)S(1)}, u32[]{:S(2)}, u32[]{:S(2)}) collective-permute-start(f32[8,16,8,128]{3,1,0,2:T(8,128)S(1)} %add.871), channel_id=1, source_target_pairs={{0,192},{64,0},{128,64},{192,128},{1,193},{65,1},{129,65},{193,129... | collective-permute-start | bytes 1572872 | tf_op jit(solution)/shard_map/ppermute | solution.py:33
  174.5 7.6 %collective-permute-start.9 = (f32[4,16,8,128]{3,1,0,2:T(8,128)S(1)}, f32[4,16,8,128]{3,1,0,2:T(8,128)S(1)}, u32[]{:S(2)}, u32[]{:S(2)}) collective-permute-start(f32[4,16,8,128]{3,1,0,2:T(8,128)S(1)} %add.859), channel_id=1, source_target_pairs={{0,8},{8,16},{16,24},{24,32},{32,40},{40,48},{48,56},{56,0},{1,9},... | collective-permute-start | bytes 786440 | tf_op jit(solution)/shard_map/ppermute | solution.py:32
  175.3 6.8 %collective-permute-start.10 = (f32[4,16,8,128]{3,1,0,2:T(8,128)S(1)}, f32[4,16,8,128]{3,1,0,2:T(8,128)S(1)}, u32[]{:S(2)}, u32[]{:S(2)}) collective-permute-start(f32[4,16,8,128]{3,1,0,2:T(8,128)S(1)} %add.863), channel_id=1, source_target_pairs={{0,56},{8,0},{16,8},{24,16},{32,24},{40,32},{48,40},{56,48},{1,57}... | collective-permute-start | bytes 786440 | tf_op jit(solution)/shard_map/ppermute | solution.py:33
  184.5 7.7 %collective-permute-start.13 = (f32[4,16,8,128]{3,1,0,2:T(8,128)S(1)}, f32[4,16,8,128]{3,1,0,2:T(8,128)S(1)}, u32[]{:S(2)}, u32[]{:S(2)}) collective-permute-start(f32[4,16,8,128]{3,1,0,2:T(8,128)S(1)} %add.875), channel_id=1, source_target_pairs={{0,8},{8,16},{16,24},{24,32},{32,40},{40,48},{48,56},{56,0},{1,9},... | collective-permute-start | bytes 786440 | tf_op jit(solution)/shard_map/ppermute | solution.py:32
  185.3 6.8 %collective-permute-start.14 = (f32[4,16,8,128]{3,1,0,2:T(8,128)S(1)}, f32[4,16,8,128]{3,1,0,2:T(8,128)S(1)}, u32[]{:S(2)}, u32[]{:S(2)}) collective-permute-start(f32[4,16,8,128]{3,1,0,2:T(8,128)S(1)} %add.879), channel_id=1, source_target_pairs={{0,56},{8,0},{16,8},{24,16},{32,24},{40,32},{48,40},{56,48},{1,57}... | collective-permute-start | bytes 786440 | tf_op jit(solution)/shard_map/ppermute | solution.py:33
  192.2 8.4 %collective-permute-start.15 = (f32[4,16,8,128]{3,1,0,2:T(8,128)S(1)}, f32[4,16,8,128]{3,1,0,2:T(8,128)S(1)}, u32[]{:S(2)}, u32[]{:S(2)}) collective-permute-start(f32[4,16,8,128]{3,1,0,2:T(8,128)S(1)} %add.888), channel_id=1, source_target_pairs={{0,8},{8,16},{16,24},{24,32},{32,40},{40,48},{48,56},{56,0},{1,9},... | collective-permute-start | bytes 786440 | tf_op jit(solution)/shard_map/ppermute | solution.py:32
  192.5 8.2 %collective-permute-start.16 = (f32[4,16,8,128]{3,1,0,2:T(8,128)S(1)}, f32[4,16,8,128]{3,1,0,2:T(8,128)S(1)}, u32[]{:S(2)}, u32[]{:S(2)}) collective-permute-start(f32[4,16,8,128]{3,1,0,2:T(8,128)S(1)} %add.892), channel_id=1, source_target_pairs={{0,56},{8,0},{16,8},{24,16},{32,24},{40,32},{48,40},{56,48},{1,57}... | collective-permute-start | bytes 786440 | tf_op jit(solution)/shard_map/ppermute | solution.py:33
  195.6 19.3 %collective-permute-start.24 = (f32[8,16,8,128]{3,1,0,2:T(8,128)S(1)}, f32[8,16,8,128]{3,1,0,2:T(8,128)S(1)}, u32[]{:S(2)}, u32[]{:S(2)}) collective-permute-start(f32[8,16,8,128]{3,1,0,2:T(8,128)S(1)} %add.884), channel_id=1, source_target_pairs={{0,192},{64,0},{128,64},{192,128},{1,193},{65,1},{129,65},{193,129... | collective-permute-start | bytes 1572872 | tf_op jit(solution)/shard_map/ppermute | solution.py:33
  199.0 26.5 %collective-permute-start.23 = (f32[8,16,8,128]{3,1,0,2:T(8,128)S(1)}, f32[8,16,8,128]{3,1,0,2:T(8,128)S(1)}, u32[]{:S(2)}, u32[]{:S(2)}) collective-permute-start(f32[8,16,8,128]{3,1,0,2:T(8,128)S(1)} %add.883), channel_id=1, source_target_pairs={{0,64},{64,128},{128,192},{192,0},{1,65},{65,129},{129,193},{193,1... | collective-permute-start | bytes 1572872 | tf_op jit(solution)/shard_map/ppermute | solution.py:32
  200.7 9.4 %collective-permute-start.17 = (f32[4,16,8,128]{3,1,0,2:T(8,128)S(1)}, f32[4,16,8,128]{3,1,0,2:T(8,128)S(1)}, u32[]{:S(2)}, u32[]{:S(2)}) collective-permute-start(f32[4,16,8,128]{3,1,0,2:T(8,128)S(1)} %add.896), channel_id=1, source_target_pairs={{0,8},{8,16},{16,24},{24,32},{32,40},{40,48},{48,56},{56,0},{1,9},... | collective-permute-start | bytes 786440 | tf_op jit(solution)/shard_map/ppermute | solution.py:32
  202.3 9.2 %collective-permute-start.18 = (f32[4,16,8,128]{3,1,0,2:T(8,128)S(1)}, f32[4,16,8,128]{3,1,0,2:T(8,128)S(1)}, u32[]{:S(2)}, u32[]{:S(2)}) collective-permute-start(f32[4,16,8,128]{3,1,0,2:T(8,128)S(1)} %add.900), channel_id=1, source_target_pairs={{0,56},{8,0},{16,8},{24,16},{32,24},{40,32},{48,40},{56,48},{1,57}... | collective-permute-start | bytes 786440 | tf_op jit(solution)/shard_map/ppermute | solution.py:33
  211.6 10.0 %collective-permute-start.19 = (f32[4,16,8,128]{3,1,0,2:T(8,128)S(1)}, f32[4,16,8,128]{3,1,0,2:T(8,128)S(1)}, u32[]{:S(2)}, u32[]{:S(2)}) collective-permute-start(f32[4,16,8,128]{3,1,0,2:T(8,128)S(1)} %add.904), channel_id=1, source_target_pairs={{0,8},{8,16},{16,24},{24,32},{32,40},{40,48},{48,56},{56,0},{1,9},... | collective-permute-start | bytes 786440 | tf_op jit(solution)/shard_map/ppermute | solution.py:32
  213.9 8.2 %collective-permute-start.20 = (f32[4,16,8,128]{3,1,0,2:T(8,128)S(1)}, f32[4,16,8,128]{3,1,0,2:T(8,128)S(1)}, u32[]{:S(2)}, u32[]{:S(2)}) collective-permute-start(f32[4,16,8,128]{3,1,0,2:T(8,128)S(1)} %add.908), channel_id=1, source_target_pairs={{0,56},{8,0},{16,8},{24,16},{32,24},{40,32},{48,40},{56,48},{1,57}... | collective-permute-start | bytes 786440 | tf_op jit(solution)/shard_map/ppermute | solution.py:33
  221.6 12.0 %copy-start.13 = (s32[2]{0:T(128)S(1)}, s32[2]{0:T(128)}, u32[]{:S(2)}) copy-start(s32[2]{0:T(128)} %param.3) | copy-start | bytes 28
  222.1 8.5 %collective-permute-start.21 = (f32[4,16,8,128]{3,1,0,2:T(8,128)S(1)}, f32[4,16,8,128]{3,1,0,2:T(8,128)S(1)}, u32[]{:S(2)}, u32[]{:S(2)}) collective-permute-start(f32[4,16,8,128]{3,1,0,2:T(8,128)S(1)} %add.912), channel_id=1, source_target_pairs={{0,8},{8,16},{16,24},{24,32},{32,40},{40,48},{48,56},{56,0},{1,9},... | collective-permute-start | bytes 786440 | tf_op jit(solution)/shard_map/ppermute | solution.py:32
  223.2 6.4 %collective-permute-start.22 = (f32[4,16,8,128]{3,1,0,2:T(8,128)S(1)}, f32[4,16,8,128]{3,1,0,2:T(8,128)S(1)}, u32[]{:S(2)}, u32[]{:S(2)}) collective-permute-start(f32[4,16,8,128]{3,1,0,2:T(8,128)S(1)} %add.913), channel_id=1, source_target_pairs={{0,56},{8,0},{16,8},{24,16},{32,24},{40,32},{48,40},{56,48},{1,57}... | collective-permute-start | bytes 786440 | tf_op jit(solution)/shard_map/ppermute | solution.py:33
  231.8 8.3 %collective-permute-start.25 = (f32[16,8,128]{2,0,1:T(8,128)S(1)}, f32[16,8,128]{2,0,1:T(8,128)S(1)}, u32[]{:S(2)}, u32[]{:S(2)}) collective-permute-start(f32[16,8,128]{2,0,1:T(8,128)S(1)} %slice.1197), channel_id=1, source_target_pairs={{0,64},{64,128},{128,192},{192,0},{1,65},{65,129},{129,193},{193,1... | collective-permute-start | bytes 196616 | tf_op jit(solution)/shard_map/ppermute | solution.py:32
  233.7 6.4 %collective-permute-start.26 = (f32[16,8,128]{2,0,1:T(8,128)S(1)}, f32[16,8,128]{2,0,1:T(8,128)S(1)}, u32[]{:S(2)}, u32[]{:S(2)}) collective-permute-start(f32[16,8,128]{2,0,1:T(8,128)S(1)} %slice.1198), channel_id=1, source_target_pairs={{0,192},{64,0},{128,64},{192,128},{1,193},{65,1},{129,65},{193,129... | collective-permute-start | bytes 196616 | tf_op jit(solution)/shard_map/ppermute | solution.py:33
  236.5 5.8 %collective-permute-start.27 = (f32[16,8,128]{2,0,1:T(8,128)S(1)}, f32[16,8,128]{2,0,1:T(8,128)S(1)}, u32[]{:S(2)}, u32[]{:S(2)}) collective-permute-start(f32[16,8,128]{2,0,1:T(8,128)S(1)} %slice.1215), channel_id=1, source_target_pairs={{0,8},{8,16},{16,24},{24,32},{32,40},{40,48},{48,56},{56,0},{1,9},... | collective-permute-start | bytes 196616 | tf_op jit(solution)/shard_map/ppermute | solution.py:32
  237.8 4.5 %collective-permute-start.28 = (f32[16,8,128]{2,0,1:T(8,128)S(1)}, f32[16,8,128]{2,0,1:T(8,128)S(1)}, u32[]{:S(2)}, u32[]{:S(2)}) collective-permute-start(f32[16,8,128]{2,0,1:T(8,128)S(1)} %slice.1216), channel_id=1, source_target_pairs={{0,56},{8,0},{16,8},{24,16},{32,24},{40,32},{48,40},{56,48},{1,57}... | collective-permute-start | bytes 196616 | tf_op jit(solution)/shard_map/ppermute | solution.py:33
  242.4 5.7 %collective-permute-start.30 = (f32[16,8,128]{2,0,1:T(8,128)S(1)}, f32[16,8,128]{2,0,1:T(8,128)S(1)}, u32[]{:S(2)}, u32[]{:S(2)}) collective-permute-start(f32[16,8,128]{2,0,1:T(8,128)S(1)} %slice_add_fusion.18), channel_id=1, source_target_pairs={{0,192},{64,0},{128,64},{192,128},{1,193},{65,1},{129,65},{193,129... | collective-permute-start | bytes 196616 | tf_op jit(solution)/shard_map/ppermute | solution.py:33
  244.6 5.6 %collective-permute-start.29 = (f32[16,8,128]{2,0,1:T(8,128)S(1)}, f32[16,8,128]{2,0,1:T(8,128)S(1)}, u32[]{:S(2)}, u32[]{:S(2)}) collective-permute-start(f32[16,8,128]{2,0,1:T(8,128)S(1)} %slice_add_fusion.19), channel_id=1, source_target_pairs={{0,64},{64,128},{128,192},{192,0},{1,65},{65,129},{129,193},{193,1... | collective-permute-start | bytes 196616 | tf_op jit(solution)/shard_map/ppermute | solution.py:32
  244.7 5.5 %collective-permute-start.31 = (f32[16,8,128]{2,0,1:T(8,128)S(1)}, f32[16,8,128]{2,0,1:T(8,128)S(1)}, u32[]{:S(2)}, u32[]{:S(2)}) collective-permute-start(f32[16,8,128]{2,0,1:T(8,128)S(1)} %slice_add_fusion.17), channel_id=1, source_target_pairs={{0,8},{8,16},{16,24},{24,32},{32,40},{40,48},{48,56},{56,0},{1,9},... | collective-permute-start | bytes 196616 | tf_op jit(solution)/shard_map/ppermute | solution.py:32
  246.0 4.3 %collective-permute-start.32 = (f32[16,8,128]{2,0,1:T(8,128)S(1)}, f32[16,8,128]{2,0,1:T(8,128)S(1)}, u32[]{:S(2)}, u32[]{:S(2)}) collective-permute-start(f32[16,8,128]{2,0,1:T(8,128)S(1)} %slice_add_fusion.16), channel_id=1, source_target_pairs={{0,56},{8,0},{16,8},{24,16},{32,24},{40,32},{48,40},{56,48},{1,57}... | collective-permute-start | bytes 196616 | tf_op jit(solution)/shard_map/ppermute | solution.py:33
  250.3 5.6 %collective-permute-start.35 = (f32[16,8,128]{2,0,1:T(8,128)S(1)}, f32[16,8,128]{2,0,1:T(8,128)S(1)}, u32[]{:S(2)}, u32[]{:S(2)}) collective-permute-start(f32[16,8,128]{2,0,1:T(8,128)S(1)} %slice_add_fusion.13), channel_id=1, source_target_pairs={{0,8},{8,16},{16,24},{24,32},{32,40},{40,48},{48,56},{56,0},{1,9},... | collective-permute-start | bytes 196616 | tf_op jit(solution)/shard_map/ppermute | solution.py:32
  252.8 4.8 %collective-permute-start.36 = (f32[16,8,128]{2,0,1:T(8,128)S(1)}, f32[16,8,128]{2,0,1:T(8,128)S(1)}, u32[]{:S(2)}, u32[]{:S(2)}) collective-permute-start(f32[16,8,128]{2,0,1:T(8,128)S(1)} %slice_add_fusion.12), channel_id=1, source_target_pairs={{0,56},{8,0},{16,8},{24,16},{32,24},{40,32},{48,40},{56,48},{1,57}... | collective-permute-start | bytes 196616 | tf_op jit(solution)/shard_map/ppermute | solution.py:33
  257.6 5.7 %collective-permute-start.37 = (f32[16,8,128]{2,0,1:T(8,128)S(1)}, f32[16,8,128]{2,0,1:T(8,128)S(1)}, u32[]{:S(2)}, u32[]{:S(2)}) collective-permute-start(f32[16,8,128]{2,0,1:T(8,128)S(1)} %slice_add_fusion.9), channel_id=1, source_target_pairs={{0,8},{8,16},{16,24},{24,32},{32,40},{40,48},{48,56},{56,0},{1,9},... | collective-permute-start | bytes 196616 | tf_op jit(solution)/shard_map/ppermute | solution.py:32
  259.0 4.3 %collective-permute-start.38 = (f32[16,8,128]{2,0,1:T(8,128)S(1)}, f32[16,8,128]{2,0,1:T(8,128)S(1)}, u32[]{:S(2)}, u32[]{:S(2)}) collective-permute-start(f32[16,8,128]{2,0,1:T(8,128)S(1)} %slice_add_fusion.8), channel_id=1, source_target_pairs={{0,56},{8,0},{16,8},{24,16},{32,24},{40,32},{48,40},{56,48},{1,57}... | collective-permute-start | bytes 196616 | tf_op jit(solution)/shard_map/ppermute | solution.py:33
  263.3 5.7 %collective-permute-start.39 = (f32[16,8,128]{2,0,1:T(8,128)S(1)}, f32[16,8,128]{2,0,1:T(8,128)S(1)}, u32[]{:S(2)}, u32[]{:S(2)}) collective-permute-start(f32[16,8,128]{2,0,1:T(8,128)S(1)} %slice_add_fusion.7), channel_id=1, source_target_pairs={{0,8},{8,16},{16,24},{24,32},{32,40},{40,48},{48,56},{56,0},{1,9},... | collective-permute-start | bytes 196616 | tf_op jit(solution)/shard_map/ppermute | solution.py:32
  264.8 4.3 %collective-permute-start.40 = (f32[16,8,128]{2,0,1:T(8,128)S(1)}, f32[16,8,128]{2,0,1:T(8,128)S(1)}, u32[]{:S(2)}, u32[]{:S(2)}) collective-permute-start(f32[16,8,128]{2,0,1:T(8,128)S(1)} %slice_add_fusion.6), channel_id=1, source_target_pairs={{0,56},{8,0},{16,8},{24,16},{32,24},{40,32},{48,40},{56,48},{1,57}... | collective-permute-start | bytes 196616 | tf_op jit(solution)/shard_map/ppermute | solution.py:33
  269.2 6.6 %collective-permute-start.42 = (f32[16,8,128]{2,0,1:T(8,128)S(1)}, f32[16,8,128]{2,0,1:T(8,128)S(1)}, u32[]{:S(2)}, u32[]{:S(2)}) collective-permute-start(f32[16,8,128]{2,0,1:T(8,128)S(1)} %slice_add_fusion.4), channel_id=1, source_target_pairs={{0,56},{8,0},{16,8},{24,16},{32,24},{40,32},{48,40},{56,48},{1,57}... | collective-permute-start | bytes 196616 | tf_op jit(solution)/shard_map/ppermute | solution.py:33
  272.3 12.2 %collective-permute-start.33 = (f32[16,8,128]{2,0,1:T(8,128)S(1)}, f32[16,8,128]{2,0,1:T(8,128)S(1)}, u32[]{:S(2)}, u32[]{:S(2)}) collective-permute-start(f32[16,8,128]{2,0,1:T(8,128)S(1)} %slice_add_fusion.15), channel_id=1, source_target_pairs={{0,64},{64,128},{128,192},{192,0},{1,65},{65,129},{129,193},{193,1... | collective-permute-start | bytes 196616 | tf_op jit(solution)/shard_map/ppermute | solution.py:32
  272.3 12.2 %collective-permute-start.34 = (f32[16,8,128]{2,0,1:T(8,128)S(1)}, f32[16,8,128]{2,0,1:T(8,128)S(1)}, u32[]{:S(2)}, u32[]{:S(2)}) collective-permute-start(f32[16,8,128]{2,0,1:T(8,128)S(1)} %slice_add_fusion.14), channel_id=1, source_target_pairs={{0,192},{64,0},{128,64},{192,128},{1,193},{65,1},{129,65},{193,129... | collective-permute-start | bytes 196616 | tf_op jit(solution)/shard_map/ppermute | solution.py:33
  275.8 5.5 %collective-permute-start.41 = (f32[16,8,128]{2,0,1:T(8,128)S(1)}, f32[16,8,128]{2,0,1:T(8,128)S(1)}, u32[]{:S(2)}, u32[]{:S(2)}) collective-permute-start(f32[16,8,128]{2,0,1:T(8,128)S(1)} %slice_add_fusion.5), channel_id=1, source_target_pairs={{0,8},{8,16},{16,24},{24,32},{32,40},{40,48},{48,56},{56,0},{1,9},... | collective-permute-start | bytes 196616 | tf_op jit(solution)/shard_map/ppermute | solution.py:32
  281.3 5.6 %collective-permute-start.43 = (f32[16,8,128]{2,0,1:T(8,128)S(1)}, f32[16,8,128]{2,0,1:T(8,128)S(1)}, u32[]{:S(2)}, u32[]{:S(2)}) collective-permute-start(f32[16,8,128]{2,0,1:T(8,128)S(1)} %slice_add_fusion.3), channel_id=1, source_target_pairs={{0,8},{8,16},{16,24},{24,32},{32,40},{40,48},{48,56},{56,0},{1,9},... | collective-permute-start | bytes 196616 | tf_op jit(solution)/shard_map/ppermute | solution.py:32
  281.3 5.5 %collective-permute-start.44 = (f32[16,8,128]{2,0,1:T(8,128)S(1)}, f32[16,8,128]{2,0,1:T(8,128)S(1)}, u32[]{:S(2)}, u32[]{:S(2)}) collective-permute-start(f32[16,8,128]{2,0,1:T(8,128)S(1)} %slice_add_fusion.2), channel_id=1, source_target_pairs={{0,56},{8,0},{16,8},{24,16},{32,24},{40,32},{48,40},{56,48},{1,57}... | collective-permute-start | bytes 196616 | tf_op jit(solution)/shard_map/ppermute | solution.py:33
  (13 other events, 62.3 us)

commit v2 on v0

--- a/solution.py
+++ b/solution.py
@@ -21,12 +21,14 @@
     me = lax.axis_index(axis)
     forward = [(i, (i + 1) % count) for i in range(count)]
     backward = [(i, (i - 1) % count) for i in range(count)]
-    up = piece_of(me - 1 + count, 0)
-    down = piece_of(me + 1, 1)
-    for step in range(count - 1):
-        up, down = lax.optimization_barrier((up, down))
+
+    def hop(step, carry):
+        up, down = lax.optimization_barrier(carry)
         up = lax.ppermute(up, axis, forward) + piece_of(me - step - 2 + 2 * count, 0)
         down = lax.ppermute(down, axis, backward) + piece_of(me + step + 2, 1)
+        return up, down
+
+    up, down = lax.fori_loop(0, count - 1, hop, (piece_of(me - 1 + count, 0), piece_of(me + 1, 1)))
     return jnp.concatenate([up, down], axis=-1)
 
 

time: 292 us -> 268 us (0.918)
  waiting for transfers between devices: 97.3 us -> 54.1 us
  local copies, waits for them, and re-layouts: 48.8 us -> 67 us
  other arithmetic: 21.8 us -> 25.4 us
    ppermute x20, waiting for transfers between devices: 97.3 us -> 54.1 us  [the longest x10 38 us: hop(): down = lax.ppermute(down, axis, backward) + piece_of(me + step + 2, 1)]
    unnamed x139 -> x24, local copies, waits for them, and re-layouts: 36.2 us -> 4.45 us
    squeeze x4 -> x32, local copies, waits for them, and re-layouts: 3.39 us -> 32.9 us  [first_piece(): lax.dynamic_index_in_dim(g, index % minor_count, 1, keepdims=False)]
    while x0 -> x59, local copies, waits for them, and re-layouts: none -> 10.1 us  [the longest x10 9.75 us: ring_steps(): lax.fori_loop(0, count - 1, hop, (piece_of(me - 1 + count, 0), piece_of(m...]
    another operation x15 -> x80, local copies, waits for them, and re-layouts: 0.74 us -> 10.3 us  [first_piece(): return jnp.stack(pieces, axis=2)]
    add x18 -> x20, other arithmetic: 2.23 us -> 6.74 us  [the longest x10 6.21 us: hop(): down = lax.ppermute(down, axis, backward) + piece_of(me + step + 2, 1)]
  transfers between devices with their start and end apart: 25 -> 25, of which waited for: 19 -> 20; matrix products, arithmetic and copies ran while one was open for 30% -> 41% of each run, Pallas kernels for 0% -> 0%
where the time goes in v2:
time: 268 us; the launch traced here: 263 us
  local copies, waits for them, and re-layouts  67 us (25%)
  waiting for transfers between devices  54.1 us (20%)
  blocking collectives  52.4 us (20%)
  matrix products  31 us (12%)
  starting transfers between devices  30.7 us (11%)
  other arithmetic  25.4 us (9%)
    psum x4, blocking collectives, samp_sum(): return lax.psum(lax.psum(value, 'samp_z'), 'samp_x')  52.4 us
    ppermute x10, waiting for transfers between devices, hop(): down = lax.ppermute(down, axis, backward) + piece_of(me + step + 2, 1)  38 us
    squeeze x32, local copies, waits for them, and re-layouts, first_piece(): lax.dynamic_index_in_dim(g, index % minor_count, 1, keepdims=False)  32.9 us
    dot_general x8, matrix products, tile(): lax.dot_general(left_panel, right_panel, transposed_dims, precision=HIGHE...  31 us
    ppermute x10, waiting for transfers between devices, hop(): lax.ppermute(up, axis, forward) + piece_of(me - step - 2 + 2 * count, 0)  16.1 us
    ppermute x10, starting transfers between devices, hop(): down = lax.ppermute(down, axis, backward) + piece_of(me + step + 2, 1)  12.7 us
    another operation x80, local copies, waits for them, and re-layouts, first_piece(): return jnp.stack(pieces, axis=2)  10.3 us
    while x10, local copies, waits for them, and re-layouts, ring_steps(): lax.fori_loop(0, count - 1, hop, (piece_of(me - 1 + count, 0), piece_of(m...  9.75 us
  transfers between devices with their start and end apart: 25, of which 20 were waited for; matrix products, arithmetic and copies ran while one was open for 41% of the time, Pallas kernels for 0%

profile of v2, /device:TPU:8, one launch (start us, length us, event | category | flops | bytes accessed | tf_op | source)
XLA Modules:
  0.0 262.9 jit_solution(240487568580224455)
XLA Ops:
  0.0 1.9 collective-permute-start.4
  1.9 3.2 %reduce_sum.18 = f32[1024]{0:T(1024)S(1)} reduce(f32[1536,1024]{1,0:T(8,128)} %param.6, f32[]{:T(128)} %constant.362.clone.1), dimensions={0}, to_apply=%region_0.0 | reduce | flops 1571840 | bytes 6295556 | tf_op jit(solution)/shard_map/reduce_sum | solution.py:85
  5.1 20.0 %psum.28 = f32[1024]{0:T(1024)S(1)} all-reduce(f32[1024]{0:T(1024)S(1)} %reduce_sum.18), channel_id=1, replica_groups=mesh['samp_x'=4,'samp_z'=8,'snp'=8] {'samp_z'}, use_global_device_ids=true, to_apply=%region_1.0 | all-reduce | flops 1024 | bytes 8192 | tf_op jit(solution)/shard_map/psum | solution.py:61
  25.1 10.5 %psum.29 = f32[1024]{0:T(1024)S(1)} all-reduce(f32[1024]{0:T(1024)S(1)} %psum.28), channel_id=1, replica_groups=mesh['samp_x'=4,'samp_z'=8,'snp'=8] {'samp_x'}, use_global_device_ids=true, to_apply=%region_2.0 | all-reduce | flops 1024 | bytes 8192 | tf_op jit(solution)/shard_map/psum | solution.py:61
  35.6 6.6 %multiply_reduce_fusion = (f32[1024]{0:T(1024)S(1)}, f32[1536,1024]{1,0:T(8,128)}) fusion(f32[1536,1024]{1,0:T(8,128)} %param.6, f32[1024]{0:T(1024)S(1)} %broadcast_multiply_fusion), kind=kLoop, calls=%fused_computation.36 | loop fusion | flops 4717568 | bytes 12591104 | tf_op jit(solution)/shard_map/reduce_sum | solution.py:88
  42.2 14.1 %psum.30 = f32[1024]{0:T(1024)S(1)} all-reduce(f32[1024]{0:T(1024)S(1)} %get-tuple-element.620), channel_id=1, replica_groups=mesh['samp_x'=4,'samp_z'=8,'snp'=8] {'samp_z'}, use_global_device_ids=true, to_apply=%region_4.0 | all-reduce | flops 1024 | bytes 8192 | tf_op jit(solution)/shard_map/psum | solution.py:61
  56.4 7.7 %psum.31 = f32[1024]{0:T(1024)S(1)} all-reduce(f32[1024]{0:T(1024)S(1)} %psum.30), channel_id=1, replica_groups=mesh['samp_x'=4,'samp_z'=8,'snp'=8] {'samp_x'}, use_global_device_ids=true, to_apply=%region_5.0 | all-reduce | flops 1024 | bytes 8192 | tf_op jit(solution)/shard_map/psum | solution.py:61
  64.1 1.9 collective-permute-start.5
  66.1 1.9 collective-permute-start.8
  68.0 2.2 slice.416
  70.2 2.3 collective-permute-start.6
  73.3 5.6 %fusion.23 = f32[512,512]{1,0:T(8,128)S(1)} fusion(f32[1536,1024]{1,0:T(8,128)} %get-tuple-element.621), kind=kOutput, calls=%fused_computation.54 | convolution fusion | flops 2415919104 | bytes 4194304 | tf_op jit(solution)/shard_map/dot_general | solution.py:107
  78.9 5.6 %fusion.21 = f32[512,512]{1,0:T(8,128)S(1)} fusion(f32[1536,1024]{1,0:T(8,128)} %get-tuple-element.621), kind=kOutput, calls=%fused_computation.52 | convolution fusion | flops 2415919104 | bytes 7340032 | tf_op jit(solution)/shard_map/dot_general | solution.py:107
  85.8 3.8 %fusion.28 = f32[512,512]{1,0:T(8,128)} fusion(f32[1536,1024]{1,0:T(8,128)S(1)} %bitcast.271), kind=kOutput, calls=%fused_computation.59 | convolution fusion | flops 2415919104 | bytes 4194304 | tf_op jit(solution)/shard_map/dot_general | solution.py:107
  92.4 2.3 copy.17
  95.4 2.4 slice.484
  97.7 1.5 collective-permute-start.7
  99.2 3.7 %broadcast_subtract_fusion = f32[1536,1024]{1,0:T(8,128)S(1)} fusion(f32[1536,1024]{1,0:T(8,128)} %collective-permute-done.4, f32[1024]{0:T(1024)S(1)} %bitcast.296), kind=kLoop, calls=%fused_computation.40 | loop fusion | flops 1572864 | bytes 12587008 | tf_op jit(solution)/shard_map/sub | solution.py:99
  102.9 2.7 %fusion.15 = f32[512,512]{1,0:T(8,128)S(1)} fusion(f32[1536,1024]{1,0:T(8,128)S(1)} %broadcast_subtract_fusion, f32[1536,1024]{1,0:T(8,128)S(1)} %bitcast.273), kind=kOutput, calls=%fused_computation.46 | convolution fusion | flops 2415919104 | bytes 7340032 | tf_op jit(solution)/shard_map/dot_general | solution.py:107
  107.9 2.7 %fusion.17 = f32[512,512]{1,0:T(8,128)S(1)} fusion(f32[1536,1024]{1,0:T(8,128)S(1)} %broadcast_subtract_fusion, f32[1536,1024]{1,0:T(8,128)S(1)} %bitcast.273), kind=kOutput, calls=%fused_computation.48 | convolution fusion | flops 2415919104 | bytes 7340032 | tf_op jit(solution)/shard_map/dot_general | solution.py:107
  111.7 2.7 %fusion.13 = f32[512,512]{1,0:T(8,128)S(1)} fusion(f32[1536,1024]{1,0:T(8,128)S(1)} %broadcast_subtract_fusion, f32[1536,1024]{1,0:T(8,128)S(1)} %bitcast.273), kind=kOutput, calls=%fused_computation.44 | convolution fusion | flops 2415919104 | bytes 7340032 | tf_op jit(solution)/shard_map/dot_general | solution.py:107
  115.7 3.0 %fusion.11 = f32[512,512]{1,0:T(8,128)S(1)} fusion(f32[1536,1024]{1,0:T(8,128)S(1)} %broadcast_subtract_fusion, f32[1536,1024]{1,0:T(8,128)S(1)} %bitcast.273), kind=kOutput, calls=%fused_computation.42 | convolution fusion | flops 2415919104 | bytes 7340032 | tf_op jit(solution)/shard_map/dot_general | solution.py:107
  122.2 4.7 %fusion.8 = f32[512,512]{1,0:T(8,128)S(1)} fusion(f32[1536,512]{1,0:T(8,128)} %collective-permute-done.6, f32[1536,512]{1,0:T(8,128)S(1)} %collective-permute-done.7, f32[1536,1024]{1,0:T(8,128)S(1)} %bitcast.273, f32[512]{0:T(512)S(1)} %bitcast.300), kind=kOutput, calls=%fused_computation.37 | convolution fusion | flops 2417491968 | bytes 10487808 | tf_op jit(solution)/shard_map/dot_general | solution.py:107
  130.3 103.5 %while.38 = (s32[]{:T(128)}, f32[4,16,8,256]{3,2,1,0:T(8,128)S(1)}, f32[4,16,8,256]{3,1,0,2:T(8,128)}, s32[]{:T(128)}, f32[4,8,16,512]{3,2,0,1:T(8,128)}, /*inde...) while((s32[]{:T(128)}, f32[4,16,8,256]{3,2,1,0:T(8,128)S(1)}, ...), condition=%wide.region_7.8_spmd, body=%wide.region_6.7_spmd.sunk | while | flops 262178 | bytes 15729251 | solution.py:31
  130.3 2.1 collective-permute-start.1
  138.5 6.2 %collective-permute-done.1 = f32[4,16,8,256]{3,1,0,2:T(8,128)S(1)} collective-permute-done((f32[4,16,8,256]{3,1,0,2:T(8,128)}, f32[4,16,8,256]{3,1,0,2:T(8,128)S(1)}, u32[]{:S(2)}, u32[]{:S(2)}) %collective-permute-start.1) | collective-permute-done | bytes 524320 | tf_op jit(solution)/shard_map/while/body/eval_jaxpr/ppermute | solution.py:28
  145.6 2.7 %collective-permute-done = f32[4,16,8,256]{3,2,1,0:T(8,128)S(1)} collective-permute-done((f32[4,16,8,256]{3,2,1,0:T(8,128)S(1)}, f32[4,16,8,256]{3,2,1,0:T(8,128)S(1)}, u32[]{:S(2)}, u32[]{:S(2)}) %collective-permute-start) | collective-permute-done | bytes 524320 | tf_op jit(solution)/shard_map/while/body/eval_jaxpr/ppermute | solution.py:27
  156.6 6.0 %collective-permute-done.1 = f32[4,16,8,256]{3,1,0,2:T(8,128)S(1)} collective-permute-done((f32[4,16,8,256]{3,1,0,2:T(8,128)}, f32[4,16,8,256]{3,1,0,2:T(8,128)S(1)}, u32[]{:S(2)}, u32[]{:S(2)}) %collective-permute-start.1) | collective-permute-done | bytes 524320 | tf_op jit(solution)/shard_map/while/body/eval_jaxpr/ppermute | solution.py:28
  172.5 5.0 %collective-permute-done.1 = f32[4,16,8,256]{3,1,0,2:T(8,128)S(1)} collective-permute-done((f32[4,16,8,256]{3,1,0,2:T(8,128)}, f32[4,16,8,256]{3,1,0,2:T(8,128)S(1)}, u32[]{:S(2)}, u32[]{:S(2)}) %collective-permute-start.1) | collective-permute-done | bytes 524320 | tf_op jit(solution)/shard_map/while/body/eval_jaxpr/ppermute | solution.py:28
  178.3 1.5 collective-permute-done
  188.1 4.1 %collective-permute-done.1 = f32[4,16,8,256]{3,1,0,2:T(8,128)S(1)} collective-permute-done((f32[4,16,8,256]{3,1,0,2:T(8,128)}, f32[4,16,8,256]{3,1,0,2:T(8,128)S(1)}, u32[]{:S(2)}, u32[]{:S(2)}) %collective-permute-start.1) | collective-permute-done | bytes 524320 | tf_op jit(solution)/shard_map/while/body/eval_jaxpr/ppermute | solution.py:28
  193.1 1.5 collective-permute-done
  202.8 3.3 %collective-permute-done.1 = f32[4,16,8,256]{3,1,0,2:T(8,128)S(1)} collective-permute-done((f32[4,16,8,256]{3,1,0,2:T(8,128)}, f32[4,16,8,256]{3,1,0,2:T(8,128)S(1)}, u32[]{:S(2)}, u32[]{:S(2)}) %collective-permute-start.1) | collective-permute-done | bytes 524320 | tf_op jit(solution)/shard_map/while/body/eval_jaxpr/ppermute | solution.py:28
  207.0 1.5 collective-permute-done
  216.7 2.4 collective-permute-done.1
  220.0 1.5 collective-permute-done
  229.8 1.5 collective-permute-done.1
  232.2 1.5 collective-permute-done
  235.3 21.4 %while.39 = (s32[]{:T(128)}, f32[16,8,256]{2,1,0:T(8,128)S(1)}, f32[16,8,256]{2,1,0:T(8,128)S(1)}, s32[]{:T(128)}, f32[4,16,8,512]{3,2,1,0:T(8,128)S(1)}, /*inde...) while((s32[]{:T(128)}, f32[16,8,256]{2,1,0:T(8,128)S(1)}, ...), condition=%wide.region_9.10_spmd, body=%wide.region_8.9_spmd.sunk | while | flops 65570 | bytes 2884115 | solution.py:31
  235.3 2.1 collective-permute-start.3
  237.5 3.6 %collective-permute-done.3 = f32[16,8,256]{2,1,0:T(8,128)S(1)} collective-permute-done((f32[16,8,256]{2,1,0:T(8,128)S(1)}, f32[16,8,256]{2,1,0:T(8,128)S(1)}, u32[]{:S(2)}, u32[]{:S(2)}) %collective-permute-start.3) | collective-permute-done | bytes 131104 | tf_op jit(solution)/shard_map/while/body/eval_jaxpr/ppermute | solution.py:28
  241.2 2.5 collective-permute-done.2
  244.1 1.8 collective-permute-start.2
  245.9 2.9 %collective-permute-done.3 = f32[16,8,256]{2,1,0:T(8,128)S(1)} collective-permute-done((f32[16,8,256]{2,1,0:T(8,128)S(1)}, f32[16,8,256]{2,1,0:T(8,128)S(1)}, u32[]{:S(2)}, u32[]{:S(2)}) %collective-permute-start.3) | collective-permute-done | bytes 131104 | tf_op jit(solution)/shard_map/while/body/eval_jaxpr/ppermute | solution.py:28
  248.8 1.5 collective-permute-done.2
  250.4 2.0 collective-permute-start.2
  252.5 2.9 %collective-permute-done.3 = f32[16,8,256]{2,1,0:T(8,128)S(1)} collective-permute-done((f32[16,8,256]{2,1,0:T(8,128)S(1)}, f32[16,8,256]{2,1,0:T(8,128)S(1)}, u32[]{:S(2)}, u32[]{:S(2)}) %collective-permute-start.3) | collective-permute-done | bytes 131104 | tf_op jit(solution)/shard_map/while/body/eval_jaxpr/ppermute | solution.py:28
  258.2 3.8 %fusion.59 = (f32[16,1,512]{2,0,1:T(8,128)S(1)}, f32[16,1,512]{2,0,1:T(8,128)S(1)}, f32[16,1,512]{2,0,1:T(8,128)S(1)}, f32[16,1,512]{2,0,1:T(8,128)S(1)}, f32[16...) fusion(f32[16,2,4,512]{3,0,2,1:T(8,128)S(1)} %bitcast.291, f32[512]{0:T(512)S(1)} %bitcast.298, f32[16]{0:T(128)S(1)} %copy-done.1, ...), kind=kLoop, calls=%fused_computation.126 | loop fusion | flops 196608 | bytes 399494 | tf_op jit(solution)/shard_map/jit(_where)/select_n | solution.py:133
  (327 shorter events, 83.6 us)
Async XLA Ops:
  0.0 95.4 %collective-permute-start.4 = (f32[1536,1024]{1,0:T(8,128)}, f32[1536,1024]{1,0:T(8,128)}, u32[]{:S(2)}, u32[]{:S(2)}) collective-permute-start(f32[1536,1024]{1,0:T(8,128)} %param.6), channel_id=1, source_target_pairs={{1,0},{2,1},{3,2},{4,3},{5,4},{6,5},{7,6},{9,8},{10,9},{11,10},{12... | collective-permute-start | bytes 18874376 | tf_op jit(solution)/shard_map/ppermute | solution.py:17
  64.1 31.2 %collective-permute-start.5 = (f32[2,1024]{1,0:T(2,128)S(1)}, f32[2,1024]{1,0:T(2,128)S(1)}, u32[]{:S(2)}, u32[]{:S(2)}) collective-permute-start(f32[2,1024]{1,0:T(2,128)S(1)} %pad_maximum_fusion.2), channel_id=1, source_target_pairs={{1,0},{2,1},{3,2},{4,3},{5,4},{6,5},{7,6},{9,8},{10,9},{11,10},{12... | collective-permute-start | bytes 24584 | tf_op jit(solution)/shard_map/ppermute | solution.py:17
  66.1 6.4 %copy-start.3 = (s32[2]{0:T(128)S(1)}, s32[2]{0:T(128)}, u32[]{:S(2)}) copy-start(s32[2]{0:T(128)} %param.7) | copy-start | bytes 28
  66.1 28.7 %collective-permute-start.8 = (f32[2,512]{1,0:T(2,128)S(1)}, f32[2,512]{1,0:T(2,128)S(1)}, u32[]{:S(2)}, u32[]{:S(2)}) collective-permute-start(f32[2,512]{1,0:T(2,128)S(1)} %fusion.72), channel_id=1, source_target_pairs={{2,0},{3,1},{4,2},{5,3},{6,4},{7,5},{10,8},{11,9},{12,10},{13,11},... | collective-permute-start | bytes 12296 | tf_op jit(solution)/shard_map/ppermute | solution.py:17
  70.2 52.0 %collective-permute-start.6 = (f32[1536,512]{1,0:T(8,128)S(1)}, f32[1536,512]{1,0:T(8,128)}, u32[]{:S(2)}, u32[]{:S(2)}) collective-permute-start(f32[1536,512]{1,0:T(8,128)S(1)} %slice.416), channel_id=1, source_target_pairs={{3,1},{5,3},{7,5},{11,9},{13,11},{15,13},{19,17},{21,19},{23,21},{... | collective-permute-start | bytes 9437192 | tf_op jit(solution)/shard_map/ppermute | solution.py:81
  73.3 12.6 %slice-start = ((s8[6291456]{0:T(1024)(128)(4,1)}), s8[4194304]{0:T(1024)(128)(4,1)S(1)}, s32[]{:S(2)}) async-start(s8[6291456]{0:T(1024)(128)(4,1)} %bitcast.270), calls=%async_computation | async-start | bytes 8388608
  78.9 7.0 %slice-start.1 = ((s8[6291456]{0:T(1024)(128)(4,1)}), s8[2097152]{0:T(1024)(128)(4,1)S(1)}, s32[]{:S(2)}) async-start(s8[6291456]{0:T(1024)(128)(4,1)} %bitcast.270), calls=%async_computation.1 | async-start | bytes 4194304
  95.4 7.5 %slice-start.2 = ((s8[6291456]{0:T(1024)(128)(4,1)}), s8[4194304]{0:T(1024)(128)(4,1)S(1)}, s32[]{:S(2)}) async-start(s8[6291456]{0:T(1024)(128)(4,1)} %bitcast.272), calls=%async_computation.2 | async-start | bytes 8388608
  97.7 24.5 %collective-permute-start.7 = (f32[1536,512]{1,0:T(8,128)S(1)}, f32[1536,512]{1,0:T(8,128)S(1)}, u32[]{:S(2)}, u32[]{:S(2)}) collective-permute-start(f32[1536,512]{1,0:T(8,128)S(1)} %slice.484), channel_id=1, source_target_pairs={{1,0},{3,2},{5,4},{7,6},{9,8},{11,10},{13,12},{15,14},{17,16},{19,... | collective-permute-start | bytes 9437192 | tf_op jit(solution)/shard_map/ppermute | solution.py:82
  99.2 3.7 %slice-start.3 = ((s8[6291456]{0:T(1024)(128)(4,1)}), s8[2097152]{0:T(1024)(128)(4,1)S(1)}, s32[]{:S(2)}) async-start(s8[6291456]{0:T(1024)(128)(4,1)} %bitcast.272), calls=%async_computation.3 | async-start | bytes 4194304
  130.3 14.5 %collective-permute-start.1 = (f32[4,16,8,256]{3,1,0,2:T(8,128)}, f32[4,16,8,256]{3,1,0,2:T(8,128)S(1)}, u32[]{:S(2)}, u32[]{:S(2)}) collective-permute-start(f32[4,16,8,256]{3,1,0,2:T(8,128)} %get-tuple-element.832), channel_id=1, source_target_pairs={{0,56},{8,0},{16,8},{24,16},{32,24},{40,32},{48,40},{56,48},{1,57}... | collective-permute-start | bytes 1572872 | tf_op jit(solution)/shard_map/while/body/eval_jaxpr/ppermute | solution.py:28
  132.4 15.9 %collective-permute-start = (f32[4,16,8,256]{3,2,1,0:T(8,128)S(1)}, f32[4,16,8,256]{3,2,1,0:T(8,128)S(1)}, u32[]{:S(2)}, u32[]{:S(2)}) collective-permute-start(f32[4,16,8,256]{3,2,1,0:T(8,128)S(1)} %get-tuple-element.823), channel_id=1, source_target_pairs={{0,8},{8,16},{16,24},{24,32},{32,40},{40,48},{48,56},{56,0},{1,9},... | collective-permute-start | bytes 1572872 | tf_op jit(solution)/shard_map/while/body/eval_jaxpr/ppermute | solution.py:27
  148.4 14.2 %collective-permute-start.1 = (f32[4,16,8,256]{3,1,0,2:T(8,128)}, f32[4,16,8,256]{3,1,0,2:T(8,128)S(1)}, u32[]{:S(2)}, u32[]{:S(2)}) collective-permute-start(f32[4,16,8,256]{3,1,0,2:T(8,128)} %get-tuple-element.832), channel_id=1, source_target_pairs={{0,56},{8,0},{16,8},{24,16},{32,24},{40,32},{48,40},{56,48},{1,57}... | collective-permute-start | bytes 1572872 | tf_op jit(solution)/shard_map/while/body/eval_jaxpr/ppermute | solution.py:28
  149.3 14.9 %collective-permute-start = (f32[4,16,8,256]{3,2,1,0:T(8,128)S(1)}, f32[4,16,8,256]{3,2,1,0:T(8,128)S(1)}, u32[]{:S(2)}, u32[]{:S(2)}) collective-permute-start(f32[4,16,8,256]{3,2,1,0:T(8,128)S(1)} %get-tuple-element.823), channel_id=1, source_target_pairs={{0,8},{8,16},{16,24},{24,32},{32,40},{40,48},{48,56},{56,0},{1,9},... | collective-permute-start | bytes 1572872 | tf_op jit(solution)/shard_map/while/body/eval_jaxpr/ppermute | solution.py:27
  164.3 13.2 %collective-permute-start.1 = (f32[4,16,8,256]{3,1,0,2:T(8,128)}, f32[4,16,8,256]{3,1,0,2:T(8,128)S(1)}, u32[]{:S(2)}, u32[]{:S(2)}) collective-permute-start(f32[4,16,8,256]{3,1,0,2:T(8,128)} %get-tuple-element.832), channel_id=1, source_target_pairs={{0,56},{8,0},{16,8},{24,16},{32,24},{40,32},{48,40},{56,48},{1,57}... | collective-permute-start | bytes 1572872 | tf_op jit(solution)/shard_map/while/body/eval_jaxpr/ppermute | solution.py:28
  165.7 14.1 %collective-permute-start = (f32[4,16,8,256]{3,2,1,0:T(8,128)S(1)}, f32[4,16,8,256]{3,2,1,0:T(8,128)S(1)}, u32[]{:S(2)}, u32[]{:S(2)}) collective-permute-start(f32[4,16,8,256]{3,2,1,0:T(8,128)S(1)} %get-tuple-element.823), channel_id=1, source_target_pairs={{0,8},{8,16},{16,24},{24,32},{32,40},{40,48},{48,56},{56,0},{1,9},... | collective-permute-start | bytes 1572872 | tf_op jit(solution)/shard_map/while/body/eval_jaxpr/ppermute | solution.py:27
  179.9 12.3 %collective-permute-start.1 = (f32[4,16,8,256]{3,1,0,2:T(8,128)}, f32[4,16,8,256]{3,1,0,2:T(8,128)S(1)}, u32[]{:S(2)}, u32[]{:S(2)}) collective-permute-start(f32[4,16,8,256]{3,1,0,2:T(8,128)} %get-tuple-element.832), channel_id=1, source_target_pairs={{0,56},{8,0},{16,8},{24,16},{32,24},{40,32},{48,40},{56,48},{1,57}... | collective-permute-start | bytes 1572872 | tf_op jit(solution)/shard_map/while/body/eval_jaxpr/ppermute | solution.py:28
  181.4 13.2 %collective-permute-start = (f32[4,16,8,256]{3,2,1,0:T(8,128)S(1)}, f32[4,16,8,256]{3,2,1,0:T(8,128)S(1)}, u32[]{:S(2)}, u32[]{:S(2)}) collective-permute-start(f32[4,16,8,256]{3,2,1,0:T(8,128)S(1)} %get-tuple-element.823), channel_id=1, source_target_pairs={{0,8},{8,16},{16,24},{24,32},{32,40},{40,48},{48,56},{56,0},{1,9},... | collective-permute-start | bytes 1572872 | tf_op jit(solution)/shard_map/while/body/eval_jaxpr/ppermute | solution.py:27
  194.7 11.4 %collective-permute-start.1 = (f32[4,16,8,256]{3,1,0,2:T(8,128)}, f32[4,16,8,256]{3,1,0,2:T(8,128)S(1)}, u32[]{:S(2)}, u32[]{:S(2)}) collective-permute-start(f32[4,16,8,256]{3,1,0,2:T(8,128)} %get-tuple-element.832), channel_id=1, source_target_pairs={{0,56},{8,0},{16,8},{24,16},{32,24},{40,32},{48,40},{56,48},{1,57}... | collective-permute-start | bytes 1572872 | tf_op jit(solution)/shard_map/while/body/eval_jaxpr/ppermute | solution.py:28
  196.1 12.4 %collective-permute-start = (f32[4,16,8,256]{3,2,1,0:T(8,128)S(1)}, f32[4,16,8,256]{3,2,1,0:T(8,128)S(1)}, u32[]{:S(2)}, u32[]{:S(2)}) collective-permute-start(f32[4,16,8,256]{3,2,1,0:T(8,128)S(1)} %get-tuple-element.823), channel_id=1, source_target_pairs={{0,8},{8,16},{16,24},{24,32},{32,40},{40,48},{48,56},{56,0},{1,9},... | collective-permute-start | bytes 1572872 | tf_op jit(solution)/shard_map/while/body/eval_jaxpr/ppermute | solution.py:27
  208.6 10.6 %collective-permute-start.1 = (f32[4,16,8,256]{3,1,0,2:T(8,128)}, f32[4,16,8,256]{3,1,0,2:T(8,128)S(1)}, u32[]{:S(2)}, u32[]{:S(2)}) collective-permute-start(f32[4,16,8,256]{3,1,0,2:T(8,128)} %get-tuple-element.832), channel_id=1, source_target_pairs={{0,56},{8,0},{16,8},{24,16},{32,24},{40,32},{48,40},{56,48},{1,57}... | collective-permute-start | bytes 1572872 | tf_op jit(solution)/shard_map/while/body/eval_jaxpr/ppermute | solution.py:28
  210.0 11.5 %collective-permute-start = (f32[4,16,8,256]{3,2,1,0:T(8,128)S(1)}, f32[4,16,8,256]{3,2,1,0:T(8,128)S(1)}, u32[]{:S(2)}, u32[]{:S(2)}) collective-permute-start(f32[4,16,8,256]{3,2,1,0:T(8,128)S(1)} %get-tuple-element.823), channel_id=1, source_target_pairs={{0,8},{8,16},{16,24},{24,32},{32,40},{40,48},{48,56},{56,0},{1,9},... | collective-permute-start | bytes 1572872 | tf_op jit(solution)/shard_map/while/body/eval_jaxpr/ppermute | solution.py:27
  221.6 9.7 %collective-permute-start.1 = (f32[4,16,8,256]{3,1,0,2:T(8,128)}, f32[4,16,8,256]{3,1,0,2:T(8,128)S(1)}, u32[]{:S(2)}, u32[]{:S(2)}) collective-permute-start(f32[4,16,8,256]{3,1,0,2:T(8,128)} %get-tuple-element.832), channel_id=1, source_target_pairs={{0,56},{8,0},{16,8},{24,16},{32,24},{40,32},{48,40},{56,48},{1,57}... | collective-permute-start | bytes 1572872 | tf_op jit(solution)/shard_map/while/body/eval_jaxpr/ppermute | solution.py:28
  223.1 10.7 %collective-permute-start = (f32[4,16,8,256]{3,2,1,0:T(8,128)S(1)}, f32[4,16,8,256]{3,2,1,0:T(8,128)S(1)}, u32[]{:S(2)}, u32[]{:S(2)}) collective-permute-start(f32[4,16,8,256]{3,2,1,0:T(8,128)S(1)} %get-tuple-element.823), channel_id=1, source_target_pairs={{0,8},{8,16},{16,24},{24,32},{32,40},{40,48},{48,56},{56,0},{1,9},... | collective-permute-start | bytes 1572872 | tf_op jit(solution)/shard_map/while/body/eval_jaxpr/ppermute | solution.py:27
  235.3 21.5 %copy-start = (f32[1,512]{1,0:T(1,128)S(1)}, f32[1,512]{1,0:T(1,128)}, u32[]{:S(2)}) copy-start(f32[1,512]{1,0:T(1,128)} %get-tuple-element.684) | copy-start | bytes 6148
  235.3 21.5 %copy-start.1 = (f32[16]{0:T(128)S(1)}, f32[16]{0:T(128)}, u32[]{:S(2)}) copy-start(f32[16]{0:T(128)} %get-tuple-element.682) | copy-start | bytes 196
  235.3 21.5 %copy-start.2 = (f32[16]{0:T(128)S(1)}, f32[16]{0:T(128)}, u32[]{:S(2)}) copy-start(f32[16]{0:T(128)} %get-tuple-element.683) | copy-start | bytes 196
  235.3 5.8 %collective-permute-start.3 = (f32[16,8,256]{2,1,0:T(8,128)S(1)}, f32[16,8,256]{2,1,0:T(8,128)S(1)}, u32[]{:S(2)}, u32[]{:S(2)}) collective-permute-start(f32[16,8,256]{2,1,0:T(8,128)S(1)} %get-tuple-element.848), channel_id=1, source_target_pairs={{0,192},{64,0},{128,64},{192,128},{1,193},{65,1},{129,65},{193,129... | collective-permute-start | bytes 393224 | tf_op jit(solution)/shard_map/while/body/eval_jaxpr/ppermute | solution.py:28
  237.4 6.3 %collective-permute-start.2 = (f32[16,8,256]{2,1,0:T(8,128)S(1)}, f32[16,8,256]{2,1,0:T(8,128)S(1)}, u32[]{:S(2)}, u32[]{:S(2)}) collective-permute-start(f32[16,8,256]{2,1,0:T(8,128)S(1)} %get-tuple-element.846), channel_id=1, source_target_pairs={{0,64},{64,128},{128,192},{192,0},{1,65},{65,129},{129,193},{193,1... | collective-permute-start | bytes 393224 | tf_op jit(solution)/shard_map/while/body/eval_jaxpr/ppermute | solution.py:27
  243.8 5.0 %collective-permute-start.3 = (f32[16,8,256]{2,1,0:T(8,128)S(1)}, f32[16,8,256]{2,1,0:T(8,128)S(1)}, u32[]{:S(2)}, u32[]{:S(2)}) collective-permute-start(f32[16,8,256]{2,1,0:T(8,128)S(1)} %get-tuple-element.848), channel_id=1, source_target_pairs={{0,192},{64,0},{128,64},{192,128},{1,193},{65,1},{129,65},{193,129... | collective-permute-start | bytes 393224 | tf_op jit(solution)/shard_map/while/body/eval_jaxpr/ppermute | solution.py:28
  244.1 6.2 %collective-permute-start.2 = (f32[16,8,256]{2,1,0:T(8,128)S(1)}, f32[16,8,256]{2,1,0:T(8,128)S(1)}, u32[]{:S(2)}, u32[]{:S(2)}) collective-permute-start(f32[16,8,256]{2,1,0:T(8,128)S(1)} %get-tuple-element.846), channel_id=1, source_target_pairs={{0,64},{64,128},{128,192},{192,0},{1,65},{65,129},{129,193},{193,1... | collective-permute-start | bytes 393224 | tf_op jit(solution)/shard_map/while/body/eval_jaxpr/ppermute | solution.py:27
  250.3 5.0 %collective-permute-start.3 = (f32[16,8,256]{2,1,0:T(8,128)S(1)}, f32[16,8,256]{2,1,0:T(8,128)S(1)}, u32[]{:S(2)}, u32[]{:S(2)}) collective-permute-start(f32[16,8,256]{2,1,0:T(8,128)S(1)} %get-tuple-element.848), channel_id=1, source_target_pairs={{0,192},{64,0},{128,64},{192,128},{1,193},{65,1},{129,65},{193,129... | collective-permute-start | bytes 393224 | tf_op jit(solution)/shard_map/while/body/eval_jaxpr/ppermute | solution.py:28
  250.4 6.2 %collective-permute-start.2 = (f32[16,8,256]{2,1,0:T(8,128)S(1)}, f32[16,8,256]{2,1,0:T(8,128)S(1)}, u32[]{:S(2)}, u32[]{:S(2)}) collective-permute-start(f32[16,8,256]{2,1,0:T(8,128)S(1)} %get-tuple-element.846), channel_id=1, source_target_pairs={{0,64},{64,128},{128,192},{192,0},{1,65},{65,129},{129,193},{193,1... | collective-permute-start | bytes 393224 | tf_op jit(solution)/shard_map/while/body/eval_jaxpr/ppermute | solution.py:27
